TPU v7x, 32 devices: a whole 2x2x4 slice. The times are simulated.
32 devices in a mesh: seq: 8 (over z, x), head: 4 (over y, core).
Axes of the slice: x: 2, y: 2, z: 4, core: 2. Of those that a mesh axis runs over, the one named last changes fastest.
Arguments:
- query_act: bfloat16 [10240, 5120], P('seq', 'head'), may hold values from -5.5 to 5.5
- key_act: bfloat16 [10240, 5120], P('seq', 'head'), may hold values from -5.5 to 5.5
- value_act: bfloat16 [10240, 5120], P('seq', 'head'), may hold values from -6 to 6
- block_lists: int32 [80, 26], P('seq'), may hold values from -1 to 79, as said below
- key_stride: int32 [4], replicated, may hold values from 1 to 8, as said below
- out_weight: bfloat16 [5120, 5120], P('head'), may hold values from -0.3125 to 0.3125
Outputs:
- layer_out: bfloat16 [10240, 5120], P('seq', 'head')
Inputs may be any that keep to these rules, and one draw needn't show every extreme that they name: `block_lists`: row i lists distinct key blocks: the 10 blocks of query block i's own frame and, for every frame at distance d of 1 to 3 on either side, max(1, 10 // 2**d) consecutive blocks of that frame; a slot holds -1 where that frame lies outside the clip. Slots stand in any order. `key_stride`: strides never fall as the distance grows; distance 0 has stride 1 and distance 3 has stride 8.
All inputs are finite; a program needn't handle non-finite values.
Results may differ from a plain program's by a relative error of at most 0.013.
Values may be sent and summed in bfloat16 or wider, within the bound.
No kernel may reach another device: no remote copies, remote signals or barrier semaphores. Data moves between devices by JAX's collectives and lax.ppermute only.
A program may use at most 192 MiB of HBM per device.

v0:
```python
import functools
import math

import jax
import jax.numpy as jnp
from jax import lax
from jax.experimental import pallas as pl
from jax.experimental.pallas import tpu as pltpu
from jax.sharding import PartitionSpec as P

HD = 128
BLK = 128
FRAME_BLK = 10
REACH = 3
FAR_STRIDE = 8


def from_behind(shard, axis, by):
    peers = lax.axis_size(axis)
    pairs = [(i, i + by) for i in range(peers) if 0 <= i + by < peers]
    return lax.ppermute(shard, axis, pairs)


def spread_far(compact, rows):
    width = compact.shape[-1]
    grown = jnp.pad(compact.reshape(rows // FAR_STRIDE, 1, width), ((0, 0), (0, FAR_STRIDE - 1), (0, 0)))
    return grown.reshape(rows, width)


def band_window(key_act, value_act, reach_dev):
    assert reach_dev == REACH == 3
    rows = key_act.shape[0]
    both = jnp.concatenate([key_act, value_act], axis=0)
    with_far = jnp.concatenate([key_act, value_act, key_act[::FAR_STRIDE], value_act[::FAR_STRIDE]], axis=0)
    half = rows // FAR_STRIDE

    def spread(got):
        return jnp.concatenate([spread_far(got[:half], rows), spread_far(got[half:], rows)], axis=0)

    up2 = from_behind(with_far, "seq", 2)
    down2 = from_behind(with_far, "seq", -2)
    up1 = from_behind(both, "seq", 1)
    down1 = from_behind(both, "seq", -1)
    up3 = from_behind(up2[2 * rows:], "seq", 1)
    down3 = from_behind(down2[2 * rows:], "seq", -1)
    pieces = [spread(up3), up2[: 2 * rows], up1, both, down1, down2[: 2 * rows], spread(down3)]
    return jnp.concatenate(pieces, axis=0)


SIDES = [(sign, d) for d in range(1, REACH + 1) for sign in (1, -1)]


def run_blocks(d):
    return max(1, FRAME_BLK // 2 ** d)


def own_kernel(q_ref, k_ref, v_ref, acc_ref, m_ref, l_ref, *, heads, scale):
    for h in range(heads):
        cols = pl.ds(h * HD, HD)
        sc = lax.dot_general(q_ref[:, cols], k_ref[:, cols], (((1,), (1,)), ((), ())), preferred_element_type=jnp.float32)
        sc = sc * scale
        m = jnp.max(sc, axis=1, keepdims=True)
        p = jnp.exp(sc - m)
        m_ref[:, h:h + 1] = m
        l_ref[:, h:h + 1] = jnp.sum(p, axis=1, keepdims=True)
        acc_ref[:, cols] = jnp.dot(p.astype(jnp.bfloat16), v_ref[:, cols], preferred_element_type=jnp.float32)


def attend_own(query, key_act, value_act):
    rows, width = query.shape
    heads = width // HD
    kernel = functools.partial(own_kernel, heads=heads, scale=1.0 / math.sqrt(HD))
    row_spec = pl.BlockSpec((BLK, width), lambda i: (i, 0))
    frame_spec = pl.BlockSpec((rows, width), lambda i: (0, 0))
    stat_spec = pl.BlockSpec((BLK, heads), lambda i: (i, 0))
    return pl.pallas_call(
        kernel,
        out_shape=(
            jax.ShapeDtypeStruct((rows, width), jnp.float32),
            jax.ShapeDtypeStruct((rows, heads), jnp.float32),
            jax.ShapeDtypeStruct((rows, heads), jnp.float32),
        ),
        grid=(rows // BLK,),
        in_specs=[row_spec, frame_spec, frame_spec],
        out_specs=(row_spec, stat_spec, stat_spec),
        compiler_params=pltpu.CompilerParams(dimension_semantics=("arbitrary",)),
        cost_estimate=pl.CostEstimate(
            flops=4 * rows * rows * width,
            transcendentals=rows * rows * heads,
            bytes_accessed=3 * rows * width * 2 + rows * width * 4,
        ),
    )(query, key_act, value_act)


def attend_kernel(t_ref, q_ref, acc1_ref, m1_ref, l1_ref, *refs, heads, scale):
    side_refs = refs[: 2 * len(SIDES)]
    mask_ref, o_ref, s_sc = refs[2 * len(SIDES):]
    chunks = []
    moff = 0
    for j, (sign, d) in enumerate(SIDES):
        n = run_blocks(d) * BLK
        chunks.append((side_refs[2 * j], side_refs[2 * j + 1], moff, n))
        moff += n
    for h in range(heads):
        cols = pl.ds(h * HD, HD)
        qh = q_ref[:, cols]
        m1 = m1_ref[:, h:h + 1]
        m = m1
        for k, v, mo, n in chunks:
            sc = lax.dot_general(qh, k[:, cols], (((1,), (1,)), ((), ())), preferred_element_type=jnp.float32)
            sc = sc * scale
            keep = mask_ref[0, :, mo:mo + n] > 0.0
            sc = jnp.where(keep, sc, -jnp.inf)
            s_sc[:, mo:mo + n] = sc
            m = jnp.maximum(m, jnp.max(sc, axis=1, keepdims=True))
        alpha = jnp.exp(m1 - m)
        total = alpha * l1_ref[:, h:h + 1]
        acc = alpha * acc1_ref[:, cols]
        for k, v, mo, n in chunks:
            p = jnp.exp(s_sc[:, mo:mo + n] - m)
            total = total + jnp.sum(p, axis=1, keepdims=True)
            acc = acc + jnp.dot(p.astype(jnp.bfloat16), v[:, cols], preferred_element_type=jnp.float32)
        o_ref[:, cols] = (acc / total).astype(o_ref.dtype)


def attend(query, own, kvwin, starts, masks, rows_here):
    acc1, m1, l1 = own
    nq = query.shape[0] // BLK
    width = query.shape[1]
    heads = width // HD
    kernel = functools.partial(attend_kernel, heads=heads, scale=1.0 / math.sqrt(HD))
    q_spec = pl.BlockSpec((BLK, width), lambda i, t: (i, 0))
    stat_spec = pl.BlockSpec((BLK, heads), lambda i, t: (i, 0))
    side_specs = []
    side_args = []
    for j, (sign, d) in enumerate(SIDES):
        n = run_blocks(d) * BLK
        kspec = pl.BlockSpec((pl.Element(n), pl.Element(width)), lambda i, t, j=j: (pl.multiple_of(t[j, i], BLK), 0))
        vspec = pl.BlockSpec(
            (pl.Element(n), pl.Element(width)), lambda i, t, j=j: (pl.multiple_of(t[j, i] + rows_here, BLK), 0)
        )
        side_specs += [kspec, vspec]
        side_args += [kvwin, kvwin]
    nmask = masks.shape[-1]
    return pl.pallas_call(
        kernel,
        out_shape=jax.ShapeDtypeStruct(query.shape, jnp.bfloat16),
        grid_spec=pltpu.PrefetchScalarGridSpec(
            num_scalar_prefetch=1,
            grid=(nq,),
            in_specs=[q_spec, q_spec, stat_spec, stat_spec] + side_specs + [pl.BlockSpec((1, 1, nmask), lambda i, t: (i, 0, 0))],
            out_specs=pl.BlockSpec((BLK, width), lambda i, t: (i, 0)),
            scratch_shapes=[pltpu.VMEM((BLK, nmask), jnp.float32)],
        ),
        compiler_params=pltpu.CompilerParams(dimension_semantics=("arbitrary",)),
        cost_estimate=pl.CostEstimate(
            flops=4 * query.shape[0] * nmask * width,
            transcendentals=query.shape[0] * nmask * heads,
            bytes_accessed=2 * nq * nmask * width * 2 + query.size * 8,
        ),
    )(starts, query, acc1, m1, l1, *side_args, masks)


def halving_scatter(attended, out_weight, axis):
    n = lax.axis_size(axis)
    me = lax.axis_index(axis)
    bits = n.bit_length() - 1
    group = out_weight.shape[1] // n

    def term(o):
        cols = lax.dynamic_slice_in_dim(out_weight, o * group, group, axis=1)
        t = jnp.dot(attended, cols, preferred_element_type=jnp.float32)
        return lax.optimization_barrier(t.astype(jnp.bfloat16)).astype(jnp.float32)

    level = term
    for b in range(bits):
        mb = (me >> b) & 1
        payload = jnp.stack([level(2 * k + 1 - mb).astype(jnp.bfloat16) for k in range(n >> (b + 1))])
        pairs = [(i, i ^ (1 << b)) for i in range(n)]
        got = lax.ppermute(payload, axis, pairs)

        def level(k, below=level, mb=mb, got=got):
            return below(2 * k + mb) + lax.dynamic_index_in_dim(got, k, axis=0, keepdims=False).astype(jnp.float32)

    return level(0).astype(jnp.bfloat16)


def shards(query_act, key_act, value_act, block_lists, key_stride, out_weight):
    rows_here = query_act.shape[0]
    blocks_here = rows_here // BLK
    assert blocks_here == FRAME_BLK
    reach_dev = REACH
    kvwin = band_window(key_act, value_act, reach_dev)

    seq_index = lax.axis_index("seq")
    first_block = (seq_index - reach_dev) * blocks_here
    my_frame = seq_index * blocks_here // FRAME_BLK
    usable = block_lists >= 0
    rel = jnp.where(usable, block_lists // FRAME_BLK - my_frame, 0)
    in_block = jnp.arange(BLK, dtype=jnp.int32)
    starts = []
    masks = []
    for sign, d in SIDES:
        picked = usable & (rel == sign * d)
        present = jnp.any(picked, axis=1)
        first = jnp.min(jnp.where(picked, block_lists, 1 << 20), axis=1)
        place = first - first_block
        row = (place // blocks_here) * (2 * rows_here) + (place % blocks_here) * BLK
        starts.append(jnp.where(present, row, 0))
        kept = (in_block % key_stride[d]) == 0
        kept = jnp.tile(kept, run_blocks(d))
        masks.append(present[:, None] & kept[None, :])
    starts = jnp.stack(starts).astype(jnp.int32)
    masks = jnp.concatenate(masks, axis=1).astype(jnp.float32)
    masks = masks[:, None, :]
    own = attend_own(query_act, key_act, value_act)
    cut = blocks_here // 2
    outs = []
    for lo, hi in ((0, cut), (cut, blocks_here)):
        part = tuple(a[lo * BLK:hi * BLK] for a in own)
        attended = attend(query_act[lo * BLK:hi * BLK], part, kvwin, starts[:, lo:hi], masks[lo:hi], rows_here)
        outs.append(halving_scatter(attended, out_weight, "head"))
    return jnp.concatenate(outs, axis=0)


def solution(mesh):
    placed = (
        P("seq", "head"),
        P("seq", "head"),
        P("seq", "head"),
        P("seq", None),
        P(),
        P("head", None),
    )
    return jax.shard_map(
        shards, mesh=mesh, in_specs=placed, out_specs=P("seq", "head"), check_vma=False
    )
```

profile of v0, /device:TPU:16, one launch (start us, length us, event | category | flops | bytes accessed | tf_op | source)
XLA Modules:
  0.0 588.0 jit_solution(6829610000848365831)
XLA Ops:
  0.0 4.6 slice.89
  4.6 4.6 slice.90
  9.3 7.9 %pad_maximum_fusion = bf16[2880,1280]{1,0:T(8,128)(2,1)} fusion(bf16[160,1280]{1,0:T(8,128)(2,1)S(1)} %slice.90, bf16[160,1280]{1,0:T(8,128)(2,1)S(1)} %slice.89, bf16[1280,1280]{1,0:T(8,128)(2,1)} %v_ref.1, bf16[1280,1280]{1,0:T(8,128)(2,1)} %k_ref.1), kind=kLoop, calls=%fused_computation | loop fusion | flops 29491200 | bytes 14745600 | tf_op jit(solution)/shard_map/concatenate | solution.py:34
  17.2 3.7 collective-permute-start
  20.9 2.4 collective-permute-start.4
  23.3 1.9 constant_dynamic-update-slice_fusion.1
  25.2 2.0 constant_dynamic-update-slice_fusion
  27.2 3.4 collective-permute-start.2
  30.6 4.8 collective-permute-start.3
  35.5 0.7 fusion.61
  40.2 0.1 fusion.50
  40.3 0.1 fusion.52
  40.5 0.2 select_reduce_fusion
  41.7 45.5 %shard_map.64 = (f32[1280,1280]{1,0:T(8,128)}, f32[1280,10]{1,0:T(8,128)}, f32[1280,10]{1,0:T(8,128)}) custom-call(bf16[1280,1280]{1,0:T(8,128)(2,1)} %q_ref.1, bf16[1280,1280]{1,0:T(8,128)(2,1)} %k_ref.1, bf16[1280,1280]{1,0:T(8,128)(2,1)} %v_ref.1), custom_call_target="tpu_custom_call" | custom-call | flops 8388608000 | bytes 16384000 | tf_op jit(solution)/shard_map/pallas_call | solution.py:76
  87.2 1.9 fusion.57
  89.2 2.1 copy-done.4
  91.3 3.1 fusion.56
  94.4 85.6 %collective-permute-done = bf16[2880,1280]{1,0:T(8,128)(2,1)} collective-permute-done((bf16[2880,1280]{1,0:T(8,128)(2,1)}, bf16[2880,1280]{1,0:T(8,128)(2,1)}, u32[]{:S(2)}, u32[]{:S(2)}) %collective-permute-start) | collective-permute-done | bytes 7372832 | tf_op jit(solution)/shard_map/ppermute | solution.py:21
  180.1 1.2 slice.111
  181.3 4.5 collective-permute-start.1
  185.8 1.2 slice.116
  187.0 2.4 collective-permute-start.5
  189.5 0.7 fusion.60
  190.1 0.7 copy.14.refs_12_
  190.8 0.6 slice.110.refs_12_
  191.4 2.4 fusion.58
  193.8 163.9 %collective-permute-done.1 = bf16[320,1280]{1,0:T(8,128)(2,1)S(1)} collective-permute-done((bf16[320,1280]{1,0:T(8,128)(2,1)S(1)}, bf16[320,1280]{1,0:T(8,128)(2,1)S(1)}, u32[]{:S(2)}, u32[]{:S(2)}) %collective-permute-start.1) | collective-permute-done | bytes 819232 | tf_op jit(solution)/shard_map/ppermute | solution.py:21
  357.7 0.6 copy.15
  358.4 0.6 copy.16
  359.1 0.6 copy.17
  359.7 0.6 copy.18
  360.4 2.4 fusion.3
  362.8 2.4 fusion.2
  365.2 6.0 %slice_dynamic-update-slice_fusion.1 = bf16[17920,1280]{1,0:T(8,128)(2,1)} fusion(bf16[17920,1280]{1,0:T(8,128)(2,1)} %fusion.2, bf16[2880,1280]{1,0:T(8,128)(2,1)} %collective-permute-done), kind=kLoop, calls=%fused_computation.2 | loop fusion | bytes 13107200
  371.3 6.1 %constant_dynamic-update-slice_fusion.5 = bf16[17920,1280]{1,0:T(8,128)(2,1)} fusion(bf16[17920,1280]{1,0:T(8,128)(2,1)} %slice_dynamic-update-slice_fusion.1, bf16[2560,1280]{1,0:T(8,128)(2,1)} %collective-permute-done.2), kind=kLoop, calls=%fused_computation.54 | loop fusion | bytes 13107200
  377.4 2.0 constant_dynamic-update-slice_fusion.4
  379.3 1.2 copy-done.3
  380.5 2.0 constant_dynamic-update-slice_fusion.3
  382.5 6.0 %constant_dynamic-update-slice_fusion.2 = bf16[17920,1280]{1,0:T(8,128)(2,1)} fusion(bf16[17920,1280]{1,0:T(8,128)(2,1)} %constant_dynamic-update-slice_fusion.3, bf16[2560,1280]{1,0:T(8,128)(2,1)} %collective-permute-done.3), kind=kLoop, calls=%fused_computation.51 | loop fusion | bytes 13107200
  388.5 6.0 %slice_dynamic-update-slice_fusion = bf16[17920,1280]{1,0:T(8,128)(2,1)} fusion(bf16[17920,1280]{1,0:T(8,128)(2,1)} %constant_dynamic-update-slice_fusion.2, bf16[2880,1280]{1,0:T(8,128)(2,1)} %collective-permute-done.4), kind=kLoop, calls=%fused_computation.1 | loop fusion | bytes 13107200
  394.4 2.4 fusion.1
  396.9 2.4 fusion.refs_0_.refs_1_.refs_2_.refs_3_.refs_4_.refs_5_.refs_6_.refs_7_.refs_8_.refs_9_.refs_10_.refs_11_
  399.3 41.6 %shard_map.65 = bf16[640,1280]{1,0:T(8,128)(2,1)} custom-call(s32[6,5]{1,0:T(8,128)} %get-tuple-element.50.t_ref, bf16[640,1280]{1,0:T(8,128)(2,1)} %get-tuple-element.32.q_ref, f32[640,1280]{1,0:T(8,128)} %get-tuple-element.30.acc1_ref, f32[640,10]{1,0:T(8,128)} %get-tuple-element.64.m1_ref, f32[640,10]{1,0:T(8,128)} %get-tuple-element.38.l1_ref, ...), custom_call_target="tpu_custom_call" | custom-call | flops 6710886400 | bytes 58982400 | tf_op jit(solution)/shard_map/pallas_call | solution.py:145
  440.9 4.8 convolution_convert_fusion.6
  445.7 4.2 convolution_convert_fusion.5
  450.0 2.0 pad_maximum_fusion.1
  452.0 42.0 %shard_map.66 = bf16[640,1280]{1,0:T(8,128)(2,1)} custom-call(s32[6,5]{1,0:T(8,128)} %get-tuple-element.51.t_ref, bf16[640,1280]{1,0:T(8,128)(2,1)} %get-tuple-element.33.q_ref, f32[640,1280]{1,0:T(8,128)} %get-tuple-element.31.acc1_ref, f32[640,10]{1,0:T(8,128)} %get-tuple-element.63.m1_ref, f32[640,10]{1,0:T(8,128)} %get-tuple-element.39.l1_ref, ...), custom_call_target="tpu_custom_call" | custom-call | flops 6710886400 | bytes 58982400 | tf_op jit(solution)/shard_map/pallas_call | solution.py:145
  493.9 4.8 convolution_convert_fusion.2
  498.8 4.2 convolution_convert_fusion.1
  503.0 0.3 pad_maximum_fusion.2
  503.3 0.6 collective-permute-start.8
  503.9 4.8 convolution_convert_fusion.4
  508.8 2.0 fusion.16
  510.8 1.6 collective-permute-start.7
  512.4 4.2 convolution_convert_fusion
  516.6 2.0 fusion.17
  518.7 0.9 collective-permute-start.9
  519.6 2.3 convolution_convert_fusion.7
  521.9 2.3 convolution_convert_fusion.3
  524.2 25.3 %collective-permute-done.7 = bf16[1,640,1280]{2,1,0:T(8,128)(2,1)S(1)} collective-permute-done((bf16[1,640,1280]{2,1,0:T(8,128)(2,1)S(1)}, bf16[1,640,1280]{2,1,0:T(8,128)(2,1)S(1)}, u32[]{:S(2)}, u32[]{:S(2)}) %collective-permute-start.7) | collective-permute-done | bytes 1638432 | tf_op jit(solution)/shard_map/ppermute | solution.py:180
  549.5 2.1 fusion.6
  551.6 32.1 %collective-permute-done.9 = bf16[1,640,1280]{2,1,0:T(8,128)(2,1)S(1)} collective-permute-done((bf16[1,640,1280]{2,1,0:T(8,128)(2,1)S(1)}, bf16[1,640,1280]{2,1,0:T(8,128)(2,1)S(1)}, u32[]{:S(2)}, u32[]{:S(2)}) %collective-permute-start.9) | collective-permute-done | bytes 1638432 | tf_op jit(solution)/shard_map/ppermute | solution.py:180
  583.8 2.1 fusion.4
  585.9 1.9 pad_maximum_fusion.3
  (57 shorter events, 1.2 us)
Async XLA Ops:
  9.3 14.0 %copy-start = (bf16[1280,1280]{1,0:T(8,128)(2,1)S(1)}, bf16[1280,1280]{1,0:T(8,128)(2,1)}, u32[]{:S(2)}) copy-start(bf16[1280,1280]{1,0:T(8,128)(2,1)} %k_ref.1) | copy-start | bytes 9830404
  17.2 8.1 %copy-start.2 = (bf16[1280,1280]{1,0:T(8,128)(2,1)S(1)}, bf16[1280,1280]{1,0:T(8,128)(2,1)}, u32[]{:S(2)}) copy-start(bf16[1280,1280]{1,0:T(8,128)(2,1)} %v_ref.1) | copy-start | bytes 9830404
  17.2 162.9 %collective-permute-start = (bf16[2880,1280]{1,0:T(8,128)(2,1)}, bf16[2880,1280]{1,0:T(8,128)(2,1)}, u32[]{:S(2)}, u32[]{:S(2)}) collective-permute-start(bf16[2880,1280]{1,0:T(8,128)(2,1)} %pad_maximum_fusion), channel_id=1, source_target_pairs={{0,8},{4,12},{8,16},{12,20},{16,24},{20,28},{1,9},{5,13},{9,17},{1... | collective-permute-start | bytes 22118408 | tf_op jit(solution)/shard_map/ppermute | solution.py:21
  20.9 164.9 %collective-permute-start.4 = (bf16[2880,1280]{1,0:T(8,128)(2,1)}, bf16[2880,1280]{1,0:T(8,128)(2,1)}, u32[]{:S(2)}, u32[]{:S(2)}) collective-permute-start(bf16[2880,1280]{1,0:T(8,128)(2,1)} %pad_maximum_fusion), channel_id=1, source_target_pairs={{8,0},{12,4},{16,8},{20,12},{24,16},{28,20},{9,1},{13,5},{17,9},{2... | collective-permute-start | bytes 22118408 | tf_op jit(solution)/shard_map/ppermute | solution.py:21
  25.2 10.3 %copy-start.11 = (s32[4]{0:T(128)S(1)}, s32[4]{0:T(128)}, u32[]{:S(2)}) copy-start(s32[4]{0:T(128)} %param.10) | copy-start | bytes 52
  25.2 15.0 %copy-start.10 = (s32[10,26]{1,0:T(8,128)S(1)}, s32[10,26]{1,0:T(8,128)}, u32[]{:S(2)}) copy-start(s32[10,26]{1,0:T(8,128)} %param.9) | copy-start | bytes 3124
  27.2 344.0 %collective-permute-start.2 = (bf16[2560,1280]{1,0:T(8,128)(2,1)}, bf16[2560,1280]{1,0:T(8,128)(2,1)}, u32[]{:S(2)}, u32[]{:S(2)}) collective-permute-start(bf16[2560,1280]{1,0:T(8,128)(2,1)} %constant_dynamic-update-slice_fusion), channel_id=1, source_target_pairs={{0,4},{4,8},{8,12},{12,16},{16,20},{20,24},{24,28},{1,5},{5,9},{9,... | collective-permute-start | bytes 19660808 | tf_op jit(solution)/shard_map/ppermute | solution.py:21
  30.6 351.8 %collective-permute-start.3 = (bf16[2560,1280]{1,0:T(8,128)(2,1)}, bf16[2560,1280]{1,0:T(8,128)(2,1)}, u32[]{:S(2)}, u32[]{:S(2)}) collective-permute-start(bf16[2560,1280]{1,0:T(8,128)(2,1)} %constant_dynamic-update-slice_fusion), channel_id=1, source_target_pairs={{4,0},{8,4},{12,8},{16,12},{20,16},{24,20},{28,24},{5,1},{9,5},{13... | collective-permute-start | bytes 19660808 | tf_op jit(solution)/shard_map/ppermute | solution.py:21
  41.7 45.5 %copy-start.5 = (bf16[1280,1280]{1,0:T(8,128)(2,1)S(1)}, bf16[1280,1280]{1,0:T(8,128)(2,1)}, u32[]{:S(2)}) copy-start(bf16[1280,1280]{1,0:T(8,128)(2,1)} %q_ref.1) | copy-start | bytes 9830404
  87.2 4.0 copy-start.4
  181.3 176.4 %collective-permute-start.1 = (bf16[320,1280]{1,0:T(8,128)(2,1)S(1)}, bf16[320,1280]{1,0:T(8,128)(2,1)S(1)}, u32[]{:S(2)}, u32[]{:S(2)}) collective-permute-start(bf16[320,1280]{1,0:T(8,128)(2,1)S(1)} %slice.111), channel_id=1, source_target_pairs={{0,4},{4,8},{8,12},{12,16},{16,20},{20,24},{24,28},{1,5},{5,9},{9,... | collective-permute-start | bytes 2457608 | tf_op jit(solution)/shard_map/ppermute | solution.py:21
  187.0 172.0 %collective-permute-start.5 = (bf16[320,1280]{1,0:T(8,128)(2,1)S(1)}, bf16[320,1280]{1,0:T(8,128)(2,1)S(1)}, u32[]{:S(2)}, u32[]{:S(2)}) collective-permute-start(bf16[320,1280]{1,0:T(8,128)(2,1)S(1)} %slice.116), channel_id=1, source_target_pairs={{4,0},{8,4},{12,8},{16,12},{20,16},{24,20},{28,24},{5,1},{9,5},{13... | collective-permute-start | bytes 2457608 | tf_op jit(solution)/shard_map/ppermute | solution.py:21
  371.3 6.1 %copy-start.1 = (bf16[1280,1280]{1,0:T(8,128)(2,1)S(1)}, bf16[1280,1280]{1,0:T(8,128)(2,1)}, u32[]{:S(2)}) copy-start(bf16[1280,1280]{1,0:T(8,128)(2,1)} %k_ref.1) | copy-start | bytes 9830404
  377.4 3.1 copy-start.3
  440.9 4.8 copy-start.6
  452.0 56.8 %collective-permute-start.6 = (bf16[2,640,1280]{2,1,0:T(8,128)(2,1)}, bf16[2,640,1280]{2,1,0:T(8,128)(2,1)}, u32[]{:S(2)}, u32[]{:S(2)}) collective-permute-start(bf16[2,640,1280]{2,1,0:T(8,128)(2,1)} %pad_maximum_fusion.1), channel_id=1, source_target_pairs={{0,1},{1,0},{2,3},{3,2},{4,5},{5,4},{6,7},{7,6},{8,9},{9,8},{10,11... | collective-permute-start | bytes 9830408 | tf_op jit(solution)/shard_map/ppermute | solution.py:180
  493.9 4.8 copy-start.8
  503.3 13.3 %collective-permute-start.8 = (bf16[2,640,1280]{2,1,0:T(8,128)(2,1)S(1)}, bf16[2,640,1280]{2,1,0:T(8,128)(2,1)}, u32[]{:S(2)}, u32[]{:S(2)}) collective-permute-start(bf16[2,640,1280]{2,1,0:T(8,128)(2,1)S(1)} %pad_maximum_fusion.2), channel_id=1, source_target_pairs={{0,1},{1,0},{2,3},{3,2},{4,5},{5,4},{6,7},{7,6},{8,9},{9,8},{10,11... | collective-permute-start | bytes 9830408 | tf_op jit(solution)/shard_map/ppermute | solution.py:180
  503.9 15.6 %slice-start = ((s8[13107200]{0:T(1024)(128)(4,1)}), s8[4194304]{0:T(1024)(128)(4,1)S(1)}, s32[]{:S(2)}) async-start(s8[13107200]{0:T(1024)(128)(4,1)} %bitcast.173), calls=%async_computation | async-start | bytes 8388608
  503.9 15.6 %slice-start.1 = ((s8[13107200]{0:T(1024)(128)(4,1)}), s8[4194304]{0:T(1024)(128)(4,1)S(1)}, s32[]{:S(2)}) async-start(s8[13107200]{0:T(1024)(128)(4,1)} %bitcast.173), calls=%async_computation.1 | async-start | bytes 8388608
  508.8 3.6 copy-start.9
  510.8 8.7 %slice-start.2 = ((s8[13107200]{0:T(1024)(128)(4,1)}), s8[4194304]{0:T(1024)(128)(4,1)S(1)}, s32[]{:S(2)}) async-start(s8[13107200]{0:T(1024)(128)(4,1)} %bitcast.173), calls=%async_computation.2 | async-start | bytes 8388608
  510.8 8.7 %slice-start.3 = ((s8[13107200]{0:T(1024)(128)(4,1)}), s8[524288]{0:T(1024)(128)(4,1)S(1)}, s32[]{:S(2)}) async-start(s8[13107200]{0:T(1024)(128)(4,1)} %bitcast.173), calls=%async_computation.3 | async-start | bytes 1048576
  510.8 38.7 %collective-permute-start.7 = (bf16[1,640,1280]{2,1,0:T(8,128)(2,1)S(1)}, bf16[1,640,1280]{2,1,0:T(8,128)(2,1)S(1)}, u32[]{:S(2)}, u32[]{:S(2)}) collective-permute-start(bf16[1,640,1280]{2,1,0:T(8,128)(2,1)S(1)} %fusion.16), channel_id=1, source_target_pairs={{0,2},{1,3},{2,0},{3,1},{4,6},{5,7},{6,4},{7,5},{8,10},{9,11},{10,... | collective-permute-start | bytes 4915208 | tf_op jit(solution)/shard_map/ppermute | solution.py:180
  516.6 2.9 copy-start.7
  518.7 65.1 %collective-permute-start.9 = (bf16[1,640,1280]{2,1,0:T(8,128)(2,1)S(1)}, bf16[1,640,1280]{2,1,0:T(8,128)(2,1)S(1)}, u32[]{:S(2)}, u32[]{:S(2)}) collective-permute-start(bf16[1,640,1280]{2,1,0:T(8,128)(2,1)S(1)} %fusion.17), channel_id=1, source_target_pairs={{0,2},{1,3},{2,0},{3,1},{4,6},{5,7},{6,4},{7,5},{8,10},{9,11},{10,... | collective-permute-start | bytes 4915208 | tf_op jit(solution)/shard_map/ppermute | solution.py:180
where the time goes:
time: 600 us; the launch traced here: 588 us
  waiting for transfers between devices  307 us (51%)
  Pallas kernels  129 us (22%)
  local copies, waits for them, and re-layouts  69.4 us (12%)
  matrix products  31.8 us (5%)
  starting transfers between devices  24.3 us (4%)
  other arithmetic  21.7 us (4%)
    ppermute x6, waiting for transfers between devices, from_behind(): return lax.ppermute(shard, axis, pairs)  250 us
    pallas_call x2, Pallas kernels, attend(): pl.pallas_call(kernel, out_shape=jax.ShapeDtypeStruct(query.shape, jnp.bf...  83.6 us
    ppermute x4, waiting for transfers between devices, halving_scatter(): got = lax.ppermute(payload, axis, pairs)  57.4 us
    pallas_call x1, Pallas kernels, attend_own(): pl.pallas_call(kernel, out_shape=(jax.ShapeDtypeStruct((rows, width), jnp...  45.5 us
    unnamed x46, local copies, waits for them, and re-layouts  43.1 us
    dot_general x8, matrix products, term(): t = jnp.dot(attended, cols, preferred_element_type=jnp.float32)  31.8 us
    ppermute x6, starting transfers between devices, from_behind(): return lax.ppermute(shard, axis, pairs)  21.3 us
  transfers between devices with their start and end apart: 10, of which 4 were waited for; matrix products, arithmetic and copies ran while one was open for 12% of the time, Pallas kernels for 15%

commit v1 on v0

--- a/solution.py
+++ b/solution.py
@@ -101,10 +101,14 @@
         n = run_blocks(d) * BLK
         chunks.append((side_refs[2 * j], side_refs[2 * j + 1], moff, n))
         moff += n
-    for h in range(heads):
-        cols = pl.ds(h * HD, HD)
+    lanes = lax.broadcasted_iota(jnp.int32, (BLK, heads), 1)
+
+    def one_head(h, carry):
+        cols = pl.ds(pl.multiple_of(h * HD, HD), HD)
         qh = q_ref[:, cols]
-        m1 = m1_ref[:, h:h + 1]
+        pick = lanes == h
+        m1 = jnp.sum(jnp.where(pick, m1_ref[...], 0.0), axis=1, keepdims=True)
+        l1 = jnp.sum(jnp.where(pick, l1_ref[...], 0.0), axis=1, keepdims=True)
         m = m1
         for k, v, mo, n in chunks:
             sc = lax.dot_general(qh, k[:, cols], (((1,), (1,)), ((), ())), preferred_element_type=jnp.float32)
@@ -114,13 +118,16 @@
             s_sc[:, mo:mo + n] = sc
             m = jnp.maximum(m, jnp.max(sc, axis=1, keepdims=True))
         alpha = jnp.exp(m1 - m)
-        total = alpha * l1_ref[:, h:h + 1]
+        total = alpha * l1
         acc = alpha * acc1_ref[:, cols]
         for k, v, mo, n in chunks:
             p = jnp.exp(s_sc[:, mo:mo + n] - m)
             total = total + jnp.sum(p, axis=1, keepdims=True)
             acc = acc + jnp.dot(p.astype(jnp.bfloat16), v[:, cols], preferred_element_type=jnp.float32)
         o_ref[:, cols] = (acc / total).astype(o_ref.dtype)
+        return carry
+
+    lax.fori_loop(0, heads, one_head, 0)
 
 
 def attend(query, own, kvwin, starts, masks, rows_here):

time: 600 us -> 606 us (1.010)
  Pallas kernels: 129 us -> 140 us
    pallas_call x2, Pallas kernels: 83.6 us -> 94.9 us  [attend(): pl.pallas_call(kernel, out_shape=jax.ShapeDtypeStruct(query.shape, jnp.bf...]
where the time goes in v1:
time: 606 us; the launch traced here: 599 us
  waiting for transfers between devices  307 us (51%)
  Pallas kernels  140 us (23%)
  local copies, waits for them, and re-layouts  69.4 us (11%)
  matrix products  31.8 us (5%)
  starting transfers between devices  24.3 us (4%)
  other arithmetic  21.7 us (4%)
    ppermute x6, waiting for transfers between devices, from_behind(): return lax.ppermute(shard, axis, pairs)  250 us
    pallas_call x2, Pallas kernels, attend(): pl.pallas_call(kernel, out_shape=jax.ShapeDtypeStruct(query.shape, jnp.bf...  94.9 us
    ppermute x4, waiting for transfers between devices, halving_scatter(): got = lax.ppermute(payload, axis, pairs)  57.5 us
    pallas_call x1, Pallas kernels, attend_own(): pl.pallas_call(kernel, out_shape=(jax.ShapeDtypeStruct((rows, width), jnp...  45.5 us
    unnamed x46, local copies, waits for them, and re-layouts  43.1 us
    dot_general x8, matrix products, term(): t = jnp.dot(attended, cols, preferred_element_type=jnp.float32)  31.8 us
    ppermute x6, starting transfers between devices, from_behind(): return lax.ppermute(shard, axis, pairs)  21.2 us
  transfers between devices with their start and end apart: 10, of which 4 were waited for; matrix products, arithmetic and copies ran while one was open for 12% of the time, Pallas kernels for 15%

profile of v1, /device:TPU:16, one launch (start us, length us, event | category | flops | bytes accessed | tf_op | source)
XLA Modules:
  0.0 599.1 jit_solution(3183492288049908529)
XLA Ops:
  0.0 4.6 slice.89
  4.6 4.6 slice.90
  9.3 7.9 %pad_maximum_fusion = bf16[2880,1280]{1,0:T(8,128)(2,1)} fusion(bf16[160,1280]{1,0:T(8,128)(2,1)S(1)} %slice.90, bf16[160,1280]{1,0:T(8,128)(2,1)S(1)} %slice.89, bf16[1280,1280]{1,0:T(8,128)(2,1)} %v_ref.1, bf16[1280,1280]{1,0:T(8,128)(2,1)} %k_ref.1), kind=kLoop, calls=%fused_computation | loop fusion | flops 29491200 | bytes 14745600 | tf_op jit(solution)/shard_map/concatenate | solution.py:34
  17.2 3.7 collective-permute-start
  20.9 2.4 collective-permute-start.4
  23.3 1.9 constant_dynamic-update-slice_fusion.1
  25.2 2.0 constant_dynamic-update-slice_fusion
  27.2 3.4 collective-permute-start.2
  30.6 4.8 collective-permute-start.3
  35.5 0.7 fusion.61
  40.2 0.1 fusion.50
  40.3 0.1 fusion.52
  40.5 0.2 select_reduce_fusion
  41.7 45.5 %shard_map.64 = (f32[1280,1280]{1,0:T(8,128)}, f32[1280,10]{1,0:T(8,128)}, f32[1280,10]{1,0:T(8,128)}) custom-call(bf16[1280,1280]{1,0:T(8,128)(2,1)} %q_ref.1, bf16[1280,1280]{1,0:T(8,128)(2,1)} %k_ref.1, bf16[1280,1280]{1,0:T(8,128)(2,1)} %v_ref.1), custom_call_target="tpu_custom_call" | custom-call | flops 8388608000 | bytes 16384000 | tf_op jit(solution)/shard_map/pallas_call | solution.py:76
  87.2 1.9 fusion.57
  89.2 2.1 copy-done.4
  91.3 3.1 fusion.56
  94.4 85.6 %collective-permute-done = bf16[2880,1280]{1,0:T(8,128)(2,1)} collective-permute-done((bf16[2880,1280]{1,0:T(8,128)(2,1)}, bf16[2880,1280]{1,0:T(8,128)(2,1)}, u32[]{:S(2)}, u32[]{:S(2)}) %collective-permute-start) | collective-permute-done | bytes 7372832 | tf_op jit(solution)/shard_map/ppermute | solution.py:21
  180.1 1.2 slice.111
  181.3 4.5 collective-permute-start.1
  185.8 1.2 slice.116
  187.0 2.4 collective-permute-start.5
  189.4 0.7 fusion.60
  190.1 0.7 copy.14.refs_12_
  190.7 0.6 slice.110.refs_12_
  191.4 2.4 fusion.58
  193.8 163.9 %collective-permute-done.1 = bf16[320,1280]{1,0:T(8,128)(2,1)S(1)} collective-permute-done((bf16[320,1280]{1,0:T(8,128)(2,1)S(1)}, bf16[320,1280]{1,0:T(8,128)(2,1)S(1)}, u32[]{:S(2)}, u32[]{:S(2)}) %collective-permute-start.1) | collective-permute-done | bytes 819232 | tf_op jit(solution)/shard_map/ppermute | solution.py:21
  357.7 0.6 copy.15
  358.4 0.6 copy.16
  359.1 0.6 copy.17
  359.7 0.6 copy.18
  360.4 2.4 fusion.3
  362.8 2.4 fusion.2
  365.2 6.0 %slice_dynamic-update-slice_fusion.1 = bf16[17920,1280]{1,0:T(8,128)(2,1)} fusion(bf16[17920,1280]{1,0:T(8,128)(2,1)} %fusion.2, bf16[2880,1280]{1,0:T(8,128)(2,1)} %collective-permute-done), kind=kLoop, calls=%fused_computation.2 | loop fusion | bytes 13107200
  371.3 6.1 %constant_dynamic-update-slice_fusion.5 = bf16[17920,1280]{1,0:T(8,128)(2,1)} fusion(bf16[17920,1280]{1,0:T(8,128)(2,1)} %slice_dynamic-update-slice_fusion.1, bf16[2560,1280]{1,0:T(8,128)(2,1)} %collective-permute-done.2), kind=kLoop, calls=%fused_computation.54 | loop fusion | bytes 13107200
  377.4 2.0 constant_dynamic-update-slice_fusion.4
  379.3 1.2 copy-done.3
  380.5 2.0 constant_dynamic-update-slice_fusion.3
  382.5 6.0 %constant_dynamic-update-slice_fusion.2 = bf16[17920,1280]{1,0:T(8,128)(2,1)} fusion(bf16[17920,1280]{1,0:T(8,128)(2,1)} %constant_dynamic-update-slice_fusion.3, bf16[2560,1280]{1,0:T(8,128)(2,1)} %collective-permute-done.3), kind=kLoop, calls=%fused_computation.51 | loop fusion | bytes 13107200
  388.5 6.0 slice_dynamic-update-slice_fusion
  394.4 2.4 fusion.1
  396.9 2.4 fusion.refs_0_.refs_1_.refs_2_.refs_3_.refs_4_.refs_5_.refs_6_.refs_7_.refs_8_.refs_9_.refs_10_.refs_11_
  399.3 47.6 %shard_map.65 = bf16[640,1280]{1,0:T(8,128)(2,1)} custom-call(s32[6,5]{1,0:T(8,128)} %get-tuple-element.50.t_ref, bf16[640,1280]{1,0:T(8,128)(2,1)} %get-tuple-element.32.q_ref, f32[640,1280]{1,0:T(8,128)} %get-tuple-element.30.acc1_ref, f32[640,10]{1,0:T(8,128)} %get-tuple-element.64.m1_ref, f32[640,10]{1,0:T(8,128)} %get-tuple-element.38.l1_ref, ...), custom_call_target="tpu_custom_call" | custom-call | flops 6710886400 | bytes 58982400 | tf_op jit(solution)/shard_map/pallas_call | solution.py:152
  446.9 4.8 convolution_convert_fusion.6
  451.7 4.2 convolution_convert_fusion.5
  455.9 2.0 pad_maximum_fusion.1
  457.9 47.3 %shard_map.66 = bf16[640,1280]{1,0:T(8,128)(2,1)} custom-call(s32[6,5]{1,0:T(8,128)} %get-tuple-element.51.t_ref, bf16[640,1280]{1,0:T(8,128)(2,1)} %get-tuple-element.33.q_ref, f32[640,1280]{1,0:T(8,128)} %get-tuple-element.31.acc1_ref, f32[640,10]{1,0:T(8,128)} %get-tuple-element.63.m1_ref, f32[640,10]{1,0:T(8,128)} %get-tuple-element.39.l1_ref, ...), custom_call_target="tpu_custom_call" | custom-call | flops 6710886400 | bytes 58982400 | tf_op jit(solution)/shard_map/pallas_call | solution.py:152
  505.2 4.8 convolution_convert_fusion.2
  510.1 4.2 convolution_convert_fusion.1
  514.3 0.3 pad_maximum_fusion.2
  514.6 0.6 collective-permute-start.8
  515.2 4.8 convolution_convert_fusion.4
  520.1 2.0 fusion.16
  522.1 1.6 collective-permute-start.7
  523.7 4.2 convolution_convert_fusion
  528.0 2.0 fusion.17
  530.0 0.8 collective-permute-start.9
  530.9 2.3 convolution_convert_fusion.7
  533.2 2.3 convolution_convert_fusion.3
  535.5 25.3 %collective-permute-done.7 = bf16[1,640,1280]{2,1,0:T(8,128)(2,1)S(1)} collective-permute-done((bf16[1,640,1280]{2,1,0:T(8,128)(2,1)S(1)}, bf16[1,640,1280]{2,1,0:T(8,128)(2,1)S(1)}, u32[]{:S(2)}, u32[]{:S(2)}) %collective-permute-start.7) | collective-permute-done | bytes 1638432 | tf_op jit(solution)/shard_map/ppermute | solution.py:187
  560.9 2.1 fusion.6
  563.0 32.1 %collective-permute-done.9 = bf16[1,640,1280]{2,1,0:T(8,128)(2,1)S(1)} collective-permute-done((bf16[1,640,1280]{2,1,0:T(8,128)(2,1)S(1)}, bf16[1,640,1280]{2,1,0:T(8,128)(2,1)S(1)}, u32[]{:S(2)}, u32[]{:S(2)}) %collective-permute-start.9) | collective-permute-done | bytes 1638432 | tf_op jit(solution)/shard_map/ppermute | solution.py:187
  595.1 2.1 fusion.4
  597.2 1.9 pad_maximum_fusion.3
  (57 shorter events, 1.2 us)
Async XLA Ops:
  9.3 14.0 %copy-start = (bf16[1280,1280]{1,0:T(8,128)(2,1)S(1)}, bf16[1280,1280]{1,0:T(8,128)(2,1)}, u32[]{:S(2)}) copy-start(bf16[1280,1280]{1,0:T(8,128)(2,1)} %k_ref.1) | copy-start | bytes 9830404
  17.2 8.1 %copy-start.2 = (bf16[1280,1280]{1,0:T(8,128)(2,1)S(1)}, bf16[1280,1280]{1,0:T(8,128)(2,1)}, u32[]{:S(2)}) copy-start(bf16[1280,1280]{1,0:T(8,128)(2,1)} %v_ref.1) | copy-start | bytes 9830404
  17.2 162.9 %collective-permute-start = (bf16[2880,1280]{1,0:T(8,128)(2,1)}, bf16[2880,1280]{1,0:T(8,128)(2,1)}, u32[]{:S(2)}, u32[]{:S(2)}) collective-permute-start(bf16[2880,1280]{1,0:T(8,128)(2,1)} %pad_maximum_fusion), channel_id=1, source_target_pairs={{0,8},{4,12},{8,16},{12,20},{16,24},{20,28},{1,9},{5,13},{9,17},{1... | collective-permute-start | bytes 22118408 | tf_op jit(solution)/shard_map/ppermute | solution.py:21
  20.9 164.9 %collective-permute-start.4 = (bf16[2880,1280]{1,0:T(8,128)(2,1)}, bf16[2880,1280]{1,0:T(8,128)(2,1)}, u32[]{:S(2)}, u32[]{:S(2)}) collective-permute-start(bf16[2880,1280]{1,0:T(8,128)(2,1)} %pad_maximum_fusion), channel_id=1, source_target_pairs={{8,0},{12,4},{16,8},{20,12},{24,16},{28,20},{9,1},{13,5},{17,9},{2... | collective-permute-start | bytes 22118408 | tf_op jit(solution)/shard_map/ppermute | solution.py:21
  25.2 10.3 %copy-start.11 = (s32[4]{0:T(128)S(1)}, s32[4]{0:T(128)}, u32[]{:S(2)}) copy-start(s32[4]{0:T(128)} %param.10) | copy-start | bytes 52
  25.2 15.0 %copy-start.10 = (s32[10,26]{1,0:T(8,128)S(1)}, s32[10,26]{1,0:T(8,128)}, u32[]{:S(2)}) copy-start(s32[10,26]{1,0:T(8,128)} %param.9) | copy-start | bytes 3124
  27.2 344.0 %collective-permute-start.2 = (bf16[2560,1280]{1,0:T(8,128)(2,1)}, bf16[2560,1280]{1,0:T(8,128)(2,1)}, u32[]{:S(2)}, u32[]{:S(2)}) collective-permute-start(bf16[2560,1280]{1,0:T(8,128)(2,1)} %constant_dynamic-update-slice_fusion), channel_id=1, source_target_pairs={{0,4},{4,8},{8,12},{12,16},{16,20},{20,24},{24,28},{1,5},{5,9},{9,... | collective-permute-start | bytes 19660808 | tf_op jit(solution)/shard_map/ppermute | solution.py:21
  30.6 351.8 %collective-permute-start.3 = (bf16[2560,1280]{1,0:T(8,128)(2,1)}, bf16[2560,1280]{1,0:T(8,128)(2,1)}, u32[]{:S(2)}, u32[]{:S(2)}) collective-permute-start(bf16[2560,1280]{1,0:T(8,128)(2,1)} %constant_dynamic-update-slice_fusion), channel_id=1, source_target_pairs={{4,0},{8,4},{12,8},{16,12},{20,16},{24,20},{28,24},{5,1},{9,5},{13... | collective-permute-start | bytes 19660808 | tf_op jit(solution)/shard_map/ppermute | solution.py:21
  41.7 45.5 %copy-start.5 = (bf16[1280,1280]{1,0:T(8,128)(2,1)S(1)}, bf16[1280,1280]{1,0:T(8,128)(2,1)}, u32[]{:S(2)}) copy-start(bf16[1280,1280]{1,0:T(8,128)(2,1)} %q_ref.1) | copy-start | bytes 9830404
  87.2 4.0 copy-start.4
  181.3 176.4 %collective-permute-start.1 = (bf16[320,1280]{1,0:T(8,128)(2,1)S(1)}, bf16[320,1280]{1,0:T(8,128)(2,1)S(1)}, u32[]{:S(2)}, u32[]{:S(2)}) collective-permute-start(bf16[320,1280]{1,0:T(8,128)(2,1)S(1)} %slice.111), channel_id=1, source_target_pairs={{0,4},{4,8},{8,12},{12,16},{16,20},{20,24},{24,28},{1,5},{5,9},{9,... | collective-permute-start | bytes 2457608 | tf_op jit(solution)/shard_map/ppermute | solution.py:21
  187.0 172.0 %collective-permute-start.5 = (bf16[320,1280]{1,0:T(8,128)(2,1)S(1)}, bf16[320,1280]{1,0:T(8,128)(2,1)S(1)}, u32[]{:S(2)}, u32[]{:S(2)}) collective-permute-start(bf16[320,1280]{1,0:T(8,128)(2,1)S(1)} %slice.116), channel_id=1, source_target_pairs={{4,0},{8,4},{12,8},{16,12},{20,16},{24,20},{28,24},{5,1},{9,5},{13... | collective-permute-start | bytes 2457608 | tf_op jit(solution)/shard_map/ppermute | solution.py:21
  371.3 6.1 %copy-start.1 = (bf16[1280,1280]{1,0:T(8,128)(2,1)S(1)}, bf16[1280,1280]{1,0:T(8,128)(2,1)}, u32[]{:S(2)}) copy-start(bf16[1280,1280]{1,0:T(8,128)(2,1)} %k_ref.1) | copy-start | bytes 9830404
  377.4 3.1 copy-start.3
  446.8 4.8 copy-start.6
  457.9 62.2 %collective-permute-start.6 = (bf16[2,640,1280]{2,1,0:T(8,128)(2,1)}, bf16[2,640,1280]{2,1,0:T(8,128)(2,1)}, u32[]{:S(2)}, u32[]{:S(2)}) collective-permute-start(bf16[2,640,1280]{2,1,0:T(8,128)(2,1)} %pad_maximum_fusion.1), channel_id=1, source_target_pairs={{0,1},{1,0},{2,3},{3,2},{4,5},{5,4},{6,7},{7,6},{8,9},{9,8},{10,11... | collective-permute-start | bytes 9830408 | tf_op jit(solution)/shard_map/ppermute | solution.py:187
  505.2 4.8 copy-start.8
  514.6 13.4 %collective-permute-start.8 = (bf16[2,640,1280]{2,1,0:T(8,128)(2,1)S(1)}, bf16[2,640,1280]{2,1,0:T(8,128)(2,1)}, u32[]{:S(2)}, u32[]{:S(2)}) collective-permute-start(bf16[2,640,1280]{2,1,0:T(8,128)(2,1)S(1)} %pad_maximum_fusion.2), channel_id=1, source_target_pairs={{0,1},{1,0},{2,3},{3,2},{4,5},{5,4},{6,7},{7,6},{8,9},{9,8},{10,11... | collective-permute-start | bytes 9830408 | tf_op jit(solution)/shard_map/ppermute | solution.py:187
  515.2 15.6 %slice-start = ((s8[13107200]{0:T(1024)(128)(4,1)}), s8[4194304]{0:T(1024)(128)(4,1)S(1)}, s32[]{:S(2)}) async-start(s8[13107200]{0:T(1024)(128)(4,1)} %bitcast.173), calls=%async_computation | async-start | bytes 8388608
  515.2 15.6 %slice-start.1 = ((s8[13107200]{0:T(1024)(128)(4,1)}), s8[4194304]{0:T(1024)(128)(4,1)S(1)}, s32[]{:S(2)}) async-start(s8[13107200]{0:T(1024)(128)(4,1)} %bitcast.173), calls=%async_computation.1 | async-start | bytes 8388608
  520.1 3.7 copy-start.9
  522.1 8.7 %slice-start.2 = ((s8[13107200]{0:T(1024)(128)(4,1)}), s8[4194304]{0:T(1024)(128)(4,1)S(1)}, s32[]{:S(2)}) async-start(s8[13107200]{0:T(1024)(128)(4,1)} %bitcast.173), calls=%async_computation.2 | async-start | bytes 8388608
  522.1 8.7 %slice-start.3 = ((s8[13107200]{0:T(1024)(128)(4,1)}), s8[524288]{0:T(1024)(128)(4,1)S(1)}, s32[]{:S(2)}) async-start(s8[13107200]{0:T(1024)(128)(4,1)} %bitcast.173), calls=%async_computation.3 | async-start | bytes 1048576
  522.1 38.7 %collective-permute-start.7 = (bf16[1,640,1280]{2,1,0:T(8,128)(2,1)S(1)}, bf16[1,640,1280]{2,1,0:T(8,128)(2,1)S(1)}, u32[]{:S(2)}, u32[]{:S(2)}) collective-permute-start(bf16[1,640,1280]{2,1,0:T(8,128)(2,1)S(1)} %fusion.16), channel_id=1, source_target_pairs={{0,2},{1,3},{2,0},{3,1},{4,6},{5,7},{6,4},{7,5},{8,10},{9,11},{10,... | collective-permute-start | bytes 4915208 | tf_op jit(solution)/shard_map/ppermute | solution.py:187
  528.0 2.9 copy-start.7
  530.0 65.1 %collective-permute-start.9 = (bf16[1,640,1280]{2,1,0:T(8,128)(2,1)S(1)}, bf16[1,640,1280]{2,1,0:T(8,128)(2,1)S(1)}, u32[]{:S(2)}, u32[]{:S(2)}) collective-permute-start(bf16[1,640,1280]{2,1,0:T(8,128)(2,1)S(1)} %fusion.17), channel_id=1, source_target_pairs={{0,2},{1,3},{2,0},{3,1},{4,6},{5,7},{6,4},{7,5},{8,10},{9,11},{10,... | collective-permute-start | bytes 4915208 | tf_op jit(solution)/shard_map/ppermute | solution.py:187

commit v2 on v0

--- a/solution.py
+++ b/solution.py
@@ -43,8 +43,7 @@
     down1 = from_behind(both, "seq", -1)
     up3 = from_behind(up2[2 * rows:], "seq", 1)
     down3 = from_behind(down2[2 * rows:], "seq", -1)
-    pieces = [spread(up3), up2[: 2 * rows], up1, both, down1, down2[: 2 * rows], spread(down3)]
-    return jnp.concatenate(pieces, axis=0)
+    return {(1, 1): down1, (-1, 1): up1, (1, 2): down2, (-1, 2): up2, (1, 3): spread(down3), (-1, 3): spread(up3)}
 
 
 SIDES = [(sign, d) for d in range(1, REACH + 1) for sign in (1, -1)]
@@ -123,7 +122,7 @@
         o_ref[:, cols] = (acc / total).astype(o_ref.dtype)
 
 
-def attend(query, own, kvwin, starts, masks, rows_here):
+def attend(query, own, sides, starts, masks, rows_here):
     acc1, m1, l1 = own
     nq = query.shape[0] // BLK
     width = query.shape[1]
@@ -140,7 +139,7 @@
             (pl.Element(n), pl.Element(width)), lambda i, t, j=j: (pl.multiple_of(t[j, i] + rows_here, BLK), 0)
         )
         side_specs += [kspec, vspec]
-        side_args += [kvwin, kvwin]
+        side_args += [sides[(sign, d)], sides[(sign, d)]]
     nmask = masks.shape[-1]
     return pl.pallas_call(
         kernel,
@@ -190,7 +189,7 @@
     blocks_here = rows_here // BLK
     assert blocks_here == FRAME_BLK
     reach_dev = REACH
-    kvwin = band_window(key_act, value_act, reach_dev)
+    sides = band_window(key_act, value_act, reach_dev)
 
     seq_index = lax.axis_index("seq")
     first_block = (seq_index - reach_dev) * blocks_here
@@ -204,9 +203,7 @@
         picked = usable & (rel == sign * d)
         present = jnp.any(picked, axis=1)
         first = jnp.min(jnp.where(picked, block_lists, 1 << 20), axis=1)
-        place = first - first_block
-        row = (place // blocks_here) * (2 * rows_here) + (place % blocks_here) * BLK
-        starts.append(jnp.where(present, row, 0))
+        starts.append(jnp.where(present, (first % blocks_here) * BLK, 0))
         kept = (in_block % key_stride[d]) == 0
         kept = jnp.tile(kept, run_blocks(d))
         masks.append(present[:, None] & kept[None, :])
@@ -218,7 +215,7 @@
     outs = []
     for lo, hi in ((0, cut), (cut, blocks_here)):
         part = tuple(a[lo * BLK:hi * BLK] for a in own)
-        attended = attend(query_act[lo * BLK:hi * BLK], part, kvwin, starts[:, lo:hi], masks[lo:hi], rows_here)
+        attended = attend(query_act[lo * BLK:hi * BLK], part, sides, starts[:, lo:hi], masks[lo:hi], rows_here)
         outs.append(halving_scatter(attended, out_weight, "head"))
     return jnp.concatenate(outs, axis=0)
 

time: 600 us -> 570 us (0.950)
  local copies, waits for them, and re-layouts: 69.4 us -> 36 us
  other arithmetic: 21.7 us -> 29.8 us
    unnamed x46 -> x31, local copies, waits for them, and re-layouts: 43.1 us -> 4.48 us
    concatenate x0 -> x2, other arithmetic: none -> 8.35 us  [spread(): jnp.concatenate([spread_far(got[:half], rows), spread_far(got[half:], row...]
  transfers between devices with their start and end apart: 10 -> 10, of which waited for: 4 -> 4; matrix products, arithmetic and copies ran while one was open for 12% -> 12% of each run, Pallas kernels for 15% -> 16%
where the time goes in v2:
time: 570 us; the launch traced here: 562 us
  waiting for transfers between devices  307 us (54%)
  Pallas kernels  129 us (23%)
  local copies, waits for them, and re-layouts  36 us (6%)
  matrix products  31.8 us (6%)
  other arithmetic  29.8 us (5%)
  starting transfers between devices  24.4 us (4%)
    ppermute x6, waiting for transfers between devices, from_behind(): return lax.ppermute(shard, axis, pairs)  249 us
    pallas_call x2, Pallas kernels, attend(): pl.pallas_call(kernel, out_shape=jax.ShapeDtypeStruct(query.shape, jnp.bf...  83.7 us
    ppermute x4, waiting for transfers between devices, halving_scatter(): got = lax.ppermute(payload, axis, pairs)  57.6 us
    pallas_call x1, Pallas kernels, attend_own(): pl.pallas_call(kernel, out_shape=(jax.ShapeDtypeStruct((rows, width), jnp...  45.4 us
    dot_general x8, matrix products, term(): t = jnp.dot(attended, cols, preferred_element_type=jnp.float32)  31.8 us
    ppermute x6, starting transfers between devices, from_behind(): return lax.ppermute(shard, axis, pairs)  21.4 us
  transfers between devices with their start and end apart: 10, of which 4 were waited for; matrix products, arithmetic and copies ran while one was open for 12% of the time, Pallas kernels for 16%

profile of v2, /device:TPU:16, one launch (start us, length us, event | category | flops | bytes accessed | tf_op | source)
XLA Modules:
  0.0 562.3 jit_solution(9229391562414644705)
XLA Ops:
  0.0 4.6 slice.83
  4.6 4.6 slice.84
  9.3 7.9 %pad_maximum_fusion = bf16[2880,1280]{1,0:T(8,128)(2,1)} fusion(bf16[160,1280]{1,0:T(8,128)(2,1)S(1)} %slice.84, bf16[160,1280]{1,0:T(8,128)(2,1)S(1)} %slice.83, bf16[1280,1280]{1,0:T(8,128)(2,1)} %v_ref.1, bf16[1280,1280]{1,0:T(8,128)(2,1)} %k_ref.1), kind=kLoop, calls=%fused_computation | loop fusion | flops 29491200 | bytes 14745600 | tf_op jit(solution)/shard_map/concatenate | solution.py:34
  17.2 3.7 collective-permute-start.3
  21.0 2.4 collective-permute-start.2
  23.3 1.9 constant_dynamic-update-slice_fusion.1
  25.2 1.9 constant_dynamic-update-slice_fusion
  27.1 6.4 %collective-permute-start = (bf16[2560,1280]{1,0:T(8,128)(2,1)}, bf16[2560,1280]{1,0:T(8,128)(2,1)}, u32[]{:S(2)}, u32[]{:S(2)}) collective-permute-start(bf16[2560,1280]{1,0:T(8,128)(2,1)} %constant_dynamic-update-slice_fusion), channel_id=1, source_target_pairs={{4,0},{8,4},{12,8},{16,12},{20,16},{24,20},{28,24},{5,1},{9,5},{13... | collective-permute-start | bytes 19660808 | tf_op jit(solution)/shard_map/ppermute | solution.py:21
  33.5 1.9 collective-permute-start.1
  35.5 0.6 fusion.45
  40.0 0.1 fusion.34
  40.1 0.1 fusion.36
  40.3 0.2 select_reduce_fusion
  40.5 0.1 reduce_or.66
  40.6 0.1 fusion.33
  40.7 0.1 fusion.31
  41.0 0.1 and_dynamic-update-slice_fusion
  41.1 0.1 constant_dynamic-update-slice_fusion.5
  41.1 0.1 constant_dynamic-update-slice_fusion.4
  41.2 0.1 constant_dynamic-update-slice_fusion.3
  41.4 2.0 fusion.41
  43.4 45.4 %shard_map.64 = (f32[1280,1280]{1,0:T(8,128)}, f32[1280,10]{1,0:T(8,128)}, f32[1280,10]{1,0:T(8,128)}) custom-call(bf16[1280,1280]{1,0:T(8,128)(2,1)} %q_ref.1, bf16[1280,1280]{1,0:T(8,128)(2,1)} %k_ref.1, bf16[1280,1280]{1,0:T(8,128)(2,1)} %v_ref.1), custom_call_target="tpu_custom_call" | custom-call | flops 8388608000 | bytes 16384000 | tf_op jit(solution)/shard_map/pallas_call | solution.py:75
  88.8 6.1 %fusion.40 = (f32[640,1280]{1,0:T(8,128)}, f32[640,1280]{1,0:T(8,128)}) fusion(f32[1280,1280]{1,0:T(8,128)} %get-tuple-element.8), kind=kLoop, calls=%fused_computation.109 | loop fusion | bytes 13107200 | tf_op jit(solution)/shard_map/slice | solution.py:217
  94.9 85.2 %collective-permute-done.3.refs_6_.refs_7_ = bf16[2880,1280]{1,0:T(8,128)(2,1)} collective-permute-done((bf16[2880,1280]{1,0:T(8,128)(2,1)}, bf16[2880,1280]{1,0:T(8,128)(2,1)}, u32[]{:S(2)}, u32[]{:S(2)}) %collective-permute-start.3) | collective-permute-done | bytes 7372832 | tf_op jit(solution)/shard_map/ppermute | solution.py:21
  180.1 1.2 slice.106
  181.3 4.5 collective-permute-start.5
  185.9 1.2 slice.103
  187.1 2.4 collective-permute-start.4
  189.5 0.7 fusion.44
  190.2 0.7 copy.11.refs_12_
  190.8 0.7 slice.102.refs_12_
  191.5 2.4 fusion.42
  193.8 163.9 %collective-permute-done.5 = bf16[320,1280]{1,0:T(8,128)(2,1)S(1)} collective-permute-done((bf16[320,1280]{1,0:T(8,128)(2,1)S(1)}, bf16[320,1280]{1,0:T(8,128)(2,1)S(1)}, u32[]{:S(2)}, u32[]{:S(2)}) %collective-permute-start.5) | collective-permute-done | bytes 819232 | tf_op jit(solution)/shard_map/ppermute | solution.py:21
  357.8 0.6 copy.14
  358.4 0.6 copy.15
  359.2 0.6 copy.12
  359.8 0.6 copy.13
  360.4 1.6 pad_bitcast_fusion
  362.0 3.2 pad_bitcast_fusion.2
  365.2 3.2 pad_maximum_fusion.2.refs_10_.refs_11_
  368.4 5.1 pad_maximum_fusion.1.refs_8_.refs_9_
  373.6 41.7 %shard_map.65 = bf16[640,1280]{1,0:T(8,128)(2,1)} custom-call(s32[6,5]{1,0:T(8,128)} %get-tuple-element.50.t_ref, bf16[640,1280]{1,0:T(8,128)(2,1)} %get-tuple-element.32.q_ref, f32[640,1280]{1,0:T(8,128)} %get-tuple-element.30.acc1_ref, f32[640,10]{1,0:T(8,128)} %get-tuple-element.64.m1_ref, f32[640,10]{1,0:T(8,128)} %get-tuple-element.38.l1_ref, ...), custom_call_target="tpu_custom_call" | custom-call | flops 6710886400 | bytes 58982400 | tf_op jit(solution)/shard_map/pallas_call | solution.py:144
  415.3 4.8 convolution_convert_fusion.6
  420.1 4.2 convolution_convert_fusion.5
  424.4 0.3 pad_maximum_fusion.3
  424.7 0.1 collective-permute-start.6
  424.8 42.0 %shard_map.66 = bf16[640,1280]{1,0:T(8,128)(2,1)} custom-call(s32[6,5]{1,0:T(8,128)} %get-tuple-element.51.t_ref, bf16[640,1280]{1,0:T(8,128)(2,1)} %get-tuple-element.33.q_ref, f32[640,1280]{1,0:T(8,128)} %get-tuple-element.31.acc1_ref, f32[640,10]{1,0:T(8,128)} %get-tuple-element.63.m1_ref, f32[640,10]{1,0:T(8,128)} %get-tuple-element.39.l1_ref, ...), custom_call_target="tpu_custom_call" | custom-call | flops 6710886400 | bytes 58982400 | tf_op jit(solution)/shard_map/pallas_call | solution.py:144
  466.8 4.8 convolution_convert_fusion.2
  471.6 4.2 convolution_convert_fusion.1
  475.9 2.0 pad_maximum_fusion.4
  477.8 0.5 collective-permute-start.8
  478.3 4.8 convolution_convert_fusion.4
  483.2 2.0 fusion.12
  485.2 1.6 collective-permute-start.7
  486.8 4.2 convolution_convert_fusion
  491.1 1.9 fusion.13
  493.0 0.9 collective-permute-start.9
  493.9 2.3 convolution_convert_fusion.7
  496.2 2.3 convolution_convert_fusion.3
  498.5 25.5 %collective-permute-done.7 = bf16[1,640,1280]{2,1,0:T(8,128)(2,1)S(1)} collective-permute-done((bf16[1,640,1280]{2,1,0:T(8,128)(2,1)S(1)}, bf16[1,640,1280]{2,1,0:T(8,128)(2,1)S(1)}, u32[]{:S(2)}, u32[]{:S(2)}) %collective-permute-start.7) | collective-permute-done | bytes 1638432 | tf_op jit(solution)/shard_map/ppermute | solution.py:179
  524.0 2.0 fusion.2
  526.0 32.2 %collective-permute-done.9 = bf16[1,640,1280]{2,1,0:T(8,128)(2,1)S(1)} collective-permute-done((bf16[1,640,1280]{2,1,0:T(8,128)(2,1)S(1)}, bf16[1,640,1280]{2,1,0:T(8,128)(2,1)S(1)}, u32[]{:S(2)}, u32[]{:S(2)}) %collective-permute-start.9) | collective-permute-done | bytes 1638432 | tf_op jit(solution)/shard_map/ppermute | solution.py:179
  558.2 2.0 fusion
  560.2 1.9 pad_maximum_fusion.5
  (45 shorter events, 0.4 us)
Async XLA Ops:
  9.3 14.0 %copy-start = (bf16[1280,1280]{1,0:T(8,128)(2,1)S(1)}, bf16[1280,1280]{1,0:T(8,128)(2,1)}, u32[]{:S(2)}) copy-start(bf16[1280,1280]{1,0:T(8,128)(2,1)} %k_ref.1) | copy-start | bytes 9830404
  17.2 8.0 %copy-start.1 = (bf16[1280,1280]{1,0:T(8,128)(2,1)S(1)}, bf16[1280,1280]{1,0:T(8,128)(2,1)}, u32[]{:S(2)}) copy-start(bf16[1280,1280]{1,0:T(8,128)(2,1)} %v_ref.1) | copy-start | bytes 9830404
  17.2 162.9 %collective-permute-start.3 = (bf16[2880,1280]{1,0:T(8,128)(2,1)}, bf16[2880,1280]{1,0:T(8,128)(2,1)}, u32[]{:S(2)}, u32[]{:S(2)}) collective-permute-start(bf16[2880,1280]{1,0:T(8,128)(2,1)} %pad_maximum_fusion), channel_id=1, source_target_pairs={{0,8},{4,12},{8,16},{12,20},{16,24},{20,28},{1,9},{5,13},{9,17},{1... | collective-permute-start | bytes 22118408 | tf_op jit(solution)/shard_map/ppermute | solution.py:21
  21.0 164.9 %collective-permute-start.2 = (bf16[2880,1280]{1,0:T(8,128)(2,1)}, bf16[2880,1280]{1,0:T(8,128)(2,1)}, u32[]{:S(2)}, u32[]{:S(2)}) collective-permute-start(bf16[2880,1280]{1,0:T(8,128)(2,1)} %pad_maximum_fusion), channel_id=1, source_target_pairs={{8,0},{12,4},{16,8},{20,12},{24,16},{28,20},{9,1},{13,5},{17,9},{2... | collective-permute-start | bytes 22118408 | tf_op jit(solution)/shard_map/ppermute | solution.py:21
  25.2 10.2 %copy-start.8 = (s32[4]{0:T(128)S(1)}, s32[4]{0:T(128)}, u32[]{:S(2)}) copy-start(s32[4]{0:T(128)} %param.10) | copy-start | bytes 52
  25.2 14.8 %copy-start.7 = (s32[10,26]{1,0:T(8,128)S(1)}, s32[10,26]{1,0:T(8,128)}, u32[]{:S(2)}) copy-start(s32[10,26]{1,0:T(8,128)} %param.9) | copy-start | bytes 3124
  25.2 16.2 %copy-start.2 = (bf16[1280,1280]{1,0:T(8,128)(2,1)S(1)}, bf16[1280,1280]{1,0:T(8,128)(2,1)}, u32[]{:S(2)}) copy-start(bf16[1280,1280]{1,0:T(8,128)(2,1)} %q_ref.1) | copy-start | bytes 9830404
  27.1 346.5 %collective-permute-start = (bf16[2560,1280]{1,0:T(8,128)(2,1)}, bf16[2560,1280]{1,0:T(8,128)(2,1)}, u32[]{:S(2)}, u32[]{:S(2)}) collective-permute-start(bf16[2560,1280]{1,0:T(8,128)(2,1)} %constant_dynamic-update-slice_fusion), channel_id=1, source_target_pairs={{4,0},{8,4},{12,8},{16,12},{20,16},{24,20},{28,24},{5,1},{9,5},{13... | collective-permute-start | bytes 19660808 | tf_op jit(solution)/shard_map/ppermute | solution.py:21
  33.5 340.1 %collective-permute-start.1 = (bf16[2560,1280]{1,0:T(8,128)(2,1)}, bf16[2560,1280]{1,0:T(8,128)(2,1)}, u32[]{:S(2)}, u32[]{:S(2)}) collective-permute-start(bf16[2560,1280]{1,0:T(8,128)(2,1)} %constant_dynamic-update-slice_fusion), channel_id=1, source_target_pairs={{0,4},{4,8},{8,12},{12,16},{16,20},{20,24},{24,28},{1,5},{5,9},{9,... | collective-permute-start | bytes 19660808 | tf_op jit(solution)/shard_map/ppermute | solution.py:21
  181.3 176.4 %collective-permute-start.5 = (bf16[320,1280]{1,0:T(8,128)(2,1)S(1)}, bf16[320,1280]{1,0:T(8,128)(2,1)S(1)}, u32[]{:S(2)}, u32[]{:S(2)}) collective-permute-start(bf16[320,1280]{1,0:T(8,128)(2,1)S(1)} %slice.106), channel_id=1, source_target_pairs={{0,4},{4,8},{8,12},{12,16},{16,20},{20,24},{24,28},{1,5},{5,9},{9,... | collective-permute-start | bytes 2457608 | tf_op jit(solution)/shard_map/ppermute | solution.py:21
  187.1 172.0 %collective-permute-start.4 = (bf16[320,1280]{1,0:T(8,128)(2,1)S(1)}, bf16[320,1280]{1,0:T(8,128)(2,1)S(1)}, u32[]{:S(2)}, u32[]{:S(2)}) collective-permute-start(bf16[320,1280]{1,0:T(8,128)(2,1)S(1)} %slice.103), channel_id=1, source_target_pairs={{4,0},{8,4},{12,8},{16,12},{20,16},{24,20},{28,24},{5,1},{9,5},{13... | collective-permute-start | bytes 2457608 | tf_op jit(solution)/shard_map/ppermute | solution.py:21
  415.3 4.8 copy-start.3
  424.7 58.5 %collective-permute-start.6 = (bf16[2,640,1280]{2,1,0:T(8,128)(2,1)S(1)}, bf16[2,640,1280]{2,1,0:T(8,128)(2,1)}, u32[]{:S(2)}, u32[]{:S(2)}) collective-permute-start(bf16[2,640,1280]{2,1,0:T(8,128)(2,1)S(1)} %pad_maximum_fusion.3), channel_id=1, source_target_pairs={{0,1},{1,0},{2,3},{3,2},{4,5},{5,4},{6,7},{7,6},{8,9},{9,8},{10,11... | collective-permute-start | bytes 9830408 | tf_op jit(solution)/shard_map/ppermute | solution.py:179
  466.8 4.8 copy-start.5
  477.8 13.2 %collective-permute-start.8 = (bf16[2,640,1280]{2,1,0:T(8,128)(2,1)}, bf16[2,640,1280]{2,1,0:T(8,128)(2,1)}, u32[]{:S(2)}, u32[]{:S(2)}) collective-permute-start(bf16[2,640,1280]{2,1,0:T(8,128)(2,1)} %pad_maximum_fusion.4), channel_id=1, source_target_pairs={{0,1},{1,0},{2,3},{3,2},{4,5},{5,4},{6,7},{7,6},{8,9},{9,8},{10,11... | collective-permute-start | bytes 9830408 | tf_op jit(solution)/shard_map/ppermute | solution.py:179
  478.3 15.5 %slice-start = ((s8[13107200]{0:T(1024)(128)(4,1)}), s8[4194304]{0:T(1024)(128)(4,1)S(1)}, s32[]{:S(2)}) async-start(s8[13107200]{0:T(1024)(128)(4,1)} %bitcast.87), calls=%async_computation | async-start | bytes 8388608
  478.3 15.5 %slice-start.1 = ((s8[13107200]{0:T(1024)(128)(4,1)}), s8[4194304]{0:T(1024)(128)(4,1)S(1)}, s32[]{:S(2)}) async-start(s8[13107200]{0:T(1024)(128)(4,1)} %bitcast.87), calls=%async_computation.1 | async-start | bytes 8388608
  483.2 3.6 copy-start.6
  485.2 8.7 %slice-start.2 = ((s8[13107200]{0:T(1024)(128)(4,1)}), s8[4194304]{0:T(1024)(128)(4,1)S(1)}, s32[]{:S(2)}) async-start(s8[13107200]{0:T(1024)(128)(4,1)} %bitcast.87), calls=%async_computation.2 | async-start | bytes 8388608
  485.2 8.6 %slice-start.3 = ((s8[13107200]{0:T(1024)(128)(4,1)}), s8[524288]{0:T(1024)(128)(4,1)S(1)}, s32[]{:S(2)}) async-start(s8[13107200]{0:T(1024)(128)(4,1)} %bitcast.87), calls=%async_computation.3 | async-start | bytes 1048576
  485.2 38.7 %collective-permute-start.7 = (bf16[1,640,1280]{2,1,0:T(8,128)(2,1)S(1)}, bf16[1,640,1280]{2,1,0:T(8,128)(2,1)S(1)}, u32[]{:S(2)}, u32[]{:S(2)}) collective-permute-start(bf16[1,640,1280]{2,1,0:T(8,128)(2,1)S(1)} %fusion.12), channel_id=1, source_target_pairs={{0,2},{1,3},{2,0},{3,1},{4,6},{5,7},{6,4},{7,5},{8,10},{9,11},{10,... | collective-permute-start | bytes 4915208 | tf_op jit(solution)/shard_map/ppermute | solution.py:179
  491.0 2.8 copy-start.4
  493.0 65.2 %collective-permute-start.9 = (bf16[1,640,1280]{2,1,0:T(8,128)(2,1)S(1)}, bf16[1,640,1280]{2,1,0:T(8,128)(2,1)S(1)}, u32[]{:S(2)}, u32[]{:S(2)}) collective-permute-start(bf16[1,640,1280]{2,1,0:T(8,128)(2,1)S(1)} %fusion.13), channel_id=1, source_target_pairs={{0,2},{1,3},{2,0},{3,1},{4,6},{5,7},{6,4},{7,5},{8,10},{9,11},{10,... | collective-permute-start | bytes 4915208 | tf_op jit(solution)/shard_map/ppermute | solution.py:179

commit v3 on v2

--- a/solution.py
+++ b/solution.py
@@ -43,7 +43,7 @@
     down1 = from_behind(both, "seq", -1)
     up3 = from_behind(up2[2 * rows:], "seq", 1)
     down3 = from_behind(down2[2 * rows:], "seq", -1)
-    return {(1, 1): down1, (-1, 1): up1, (1, 2): down2, (-1, 2): up2, (1, 3): spread(down3), (-1, 3): spread(up3)}
+    return {(1, 1): down1, (-1, 1): up1, (1, 2): down2, (-1, 2): up2, (1, 3): down3, (-1, 3): up3}
 
 
 SIDES = [(sign, d) for d in range(1, REACH + 1) for sign in (1, -1)]
@@ -51,6 +51,13 @@
 
 def run_blocks(d):
     return max(1, FRAME_BLK // 2 ** d)
+
+
+def side_geometry(d, rows_here):
+    unit = BLK // FAR_STRIDE if d == REACH else BLK
+    keys = run_blocks(d) * unit
+    shift = rows_here // FAR_STRIDE if d == REACH else rows_here
+    return unit, keys, shift, -(-keys // BLK) * BLK
 
 
 def own_kernel(q_ref, k_ref, v_ref, acc_ref, m_ref, l_ref, *, heads, scale):
@@ -91,15 +98,15 @@
     )(query, key_act, value_act)
 
 
-def attend_kernel(t_ref, q_ref, acc1_ref, m1_ref, l1_ref, *refs, heads, scale):
+def attend_kernel(t_ref, q_ref, acc1_ref, m1_ref, l1_ref, *refs, heads, scale, rows_here):
     side_refs = refs[: 2 * len(SIDES)]
     mask_ref, o_ref, s_sc = refs[2 * len(SIDES):]
     chunks = []
     moff = 0
     for j, (sign, d) in enumerate(SIDES):
-        n = run_blocks(d) * BLK
+        _, n, _, slot = side_geometry(d, rows_here)
         chunks.append((side_refs[2 * j], side_refs[2 * j + 1], moff, n))
-        moff += n
+        moff += slot
     for h in range(heads):
         cols = pl.ds(h * HD, HD)
         qh = q_ref[:, cols]
@@ -127,16 +134,18 @@
     nq = query.shape[0] // BLK
     width = query.shape[1]
     heads = width // HD
-    kernel = functools.partial(attend_kernel, heads=heads, scale=1.0 / math.sqrt(HD))
+    kernel = functools.partial(attend_kernel, heads=heads, scale=1.0 / math.sqrt(HD), rows_here=rows_here)
     q_spec = pl.BlockSpec((BLK, width), lambda i, t: (i, 0))
     stat_spec = pl.BlockSpec((BLK, heads), lambda i, t: (i, 0))
     side_specs = []
     side_args = []
     for j, (sign, d) in enumerate(SIDES):
-        n = run_blocks(d) * BLK
-        kspec = pl.BlockSpec((pl.Element(n), pl.Element(width)), lambda i, t, j=j: (pl.multiple_of(t[j, i], BLK), 0))
+        unit, n, shift, _ = side_geometry(d, rows_here)
+        kspec = pl.BlockSpec(
+            (pl.Element(n), pl.Element(width)), lambda i, t, j=j, u=unit: (pl.multiple_of(t[j, i], u), 0)
+        )
         vspec = pl.BlockSpec(
-            (pl.Element(n), pl.Element(width)), lambda i, t, j=j: (pl.multiple_of(t[j, i] + rows_here, BLK), 0)
+            (pl.Element(n), pl.Element(width)), lambda i, t, j=j, u=unit, s=shift: (pl.multiple_of(t[j, i] + s, u), 0)
         )
         side_specs += [kspec, vspec]
         side_args += [sides[(sign, d)], sides[(sign, d)]]
@@ -203,9 +212,12 @@
         picked = usable & (rel == sign * d)
         present = jnp.any(picked, axis=1)
         first = jnp.min(jnp.where(picked, block_lists, 1 << 20), axis=1)
-        starts.append(jnp.where(present, (first % blocks_here) * BLK, 0))
-        kept = (in_block % key_stride[d]) == 0
-        kept = jnp.tile(kept, run_blocks(d))
+        unit, n, _, slot = side_geometry(d, rows_here)
+        starts.append(jnp.where(present, (first % blocks_here) * unit, 0))
+        if d == REACH:
+            kept = jnp.arange(slot) < n
+        else:
+            kept = jnp.tile((in_block % key_stride[d]) == 0, run_blocks(d))
         masks.append(present[:, None] & kept[None, :])
     starts = jnp.stack(starts).astype(jnp.int32)
     masks = jnp.concatenate(masks, axis=1).astype(jnp.float32)

time: 570 us -> 559 us (0.981); the launches traced: 562 us -> 559 us
  Pallas kernels: 129 us -> 140 us
  local copies, waits for them, and re-layouts: 36 us -> 27.1 us
  other arithmetic: 29.8 us -> 21.4 us
    pallas_call x2, Pallas kernels: 83.7 us -> 94.7 us  [attend(): pl.pallas_call(kernel, out_shape=jax.ShapeDtypeStruct(query.shape, jnp.bf...]
    concatenate x2 -> x0, other arithmetic: 8.35 us -> none  [spread(): jnp.concatenate([spread_far(got[:half], rows), spread_far(got[half:], row...]
  transfers between devices with their start and end apart: 10 -> 10, of which waited for: 4 -> 6; matrix products, arithmetic and copies ran while one was open for 12% -> 9% of each run, Pallas kernels for 16% -> 18%
where the time goes in v3:
time: 559 us
  waiting for transfers between devices  311 us (56%)
  Pallas kernels  140 us (25%)
  matrix products  31.8 us (6%)
  local copies, waits for them, and re-layouts  27.1 us (5%)
  starting transfers between devices  24.7 us (4%)
  other arithmetic  21.4 us (4%)
    ppermute x6, waiting for transfers between devices, from_behind(): return lax.ppermute(shard, axis, pairs)  253 us
    pallas_call x2, Pallas kernels, attend(): pl.pallas_call(kernel, out_shape=jax.ShapeDtypeStruct(query.shape, jnp.bf...  94.7 us
    ppermute x4, waiting for transfers between devices, halving_scatter(): got = lax.ppermute(payload, axis, pairs)  57.6 us
    pallas_call x1, Pallas kernels, attend_own(): pl.pallas_call(kernel, out_shape=(jax.ShapeDtypeStruct((rows, width), jnp...  45.5 us
    dot_general x8, matrix products, term(): t = jnp.dot(attended, cols, preferred_element_type=jnp.float32)  31.8 us
    ppermute x6, starting transfers between devices, from_behind(): return lax.ppermute(shard, axis, pairs)  21.7 us
  transfers between devices with their start and end apart: 10, of which 6 were waited for; matrix products, arithmetic and copies ran while one was open for 9% of the time, Pallas kernels for 18%

profile of v3, /device:TPU:16, one launch (start us, length us, event | category | flops | bytes accessed | tf_op | source)
XLA Modules:
  0.0 559.5 jit_solution(13859511740062742000)
XLA Ops:
  0.0 4.6 slice.67
  4.6 4.6 slice.68
  9.3 0.0 copy-start
  9.3 7.9 %pad_maximum_fusion = bf16[2880,1280]{1,0:T(8,128)(2,1)} fusion(bf16[160,1280]{1,0:T(8,128)(2,1)S(1)} %slice.68, bf16[160,1280]{1,0:T(8,128)(2,1)S(1)} %slice.67, bf16[1280,1280]{1,0:T(8,128)(2,1)} %v_ref.1, bf16[1280,1280]{1,0:T(8,128)(2,1)} %k_ref.1), kind=kLoop, calls=%fused_computation | loop fusion | flops 29491200 | bytes 14745600 | tf_op jit(solution)/shard_map/concatenate | solution.py:34
  17.2 2.6 collective-permute-start.2
  19.8 6.4 %collective-permute-start.3 = (bf16[2880,1280]{1,0:T(8,128)(2,1)}, bf16[2880,1280]{1,0:T(8,128)(2,1)}, u32[]{:S(2)}, u32[]{:S(2)}) collective-permute-start(bf16[2880,1280]{1,0:T(8,128)(2,1)} %pad_maximum_fusion), channel_id=1, source_target_pairs={{0,8},{4,12},{8,16},{12,20},{16,24},{20,28},{1,9},{5,13},{9,17},{1... | collective-permute-start | bytes 22118408 | tf_op jit(solution)/shard_map/ppermute | solution.py:21
  26.2 1.9 constant_dynamic-update-slice_fusion.1
  28.2 2.0 constant_dynamic-update-slice_fusion
  30.1 1.9 collective-permute-start
  32.0 3.9 collective-permute-start.1
  36.0 0.7 fusion.44
  39.3 0.1 fusion.33
  39.4 0.1 fusion.35
  39.5 0.2 select_reduce_fusion
  39.7 0.1 reduce_or.66
  39.9 0.1 fusion.31
  40.0 0.1 and_dynamic-update-slice_fusion.1
  40.1 0.1 and_dynamic-update-slice_fusion
  40.2 0.1 constant_dynamic-update-slice_fusion.5
  40.3 0.1 constant_dynamic-update-slice_fusion.4
  40.3 0.1 constant_dynamic-update-slice_fusion.3
  40.4 0.1 constant_dynamic-update-slice_fusion.2
  40.5 0.7 copy.7.refs_12_
  41.2 0.6 slice.81.refs_12_
  41.9 0.7 fusion.43
  42.6 45.5 %shard_map.64 = (f32[1280,1280]{1,0:T(8,128)}, f32[1280,10]{1,0:T(8,128)}, f32[1280,10]{1,0:T(8,128)}) custom-call(bf16[1280,1280]{1,0:T(8,128)(2,1)} %q_ref.1, bf16[1280,1280]{1,0:T(8,128)(2,1)} %k_ref.1, bf16[1280,1280]{1,0:T(8,128)(2,1)} %v_ref.1), custom_call_target="tpu_custom_call" | custom-call | flops 8388608000 | bytes 16384000 | tf_op jit(solution)/shard_map/pallas_call | solution.py:82
  88.1 2.5 fusion.41
  90.6 1.9 fusion.40
  92.6 88.7 %collective-permute-done.2.refs_4_.refs_5_ = bf16[2880,1280]{1,0:T(8,128)(2,1)} collective-permute-done((bf16[2880,1280]{1,0:T(8,128)(2,1)}, bf16[2880,1280]{1,0:T(8,128)(2,1)}, u32[]{:S(2)}, u32[]{:S(2)}) %collective-permute-start.2) | collective-permute-done | bytes 7372832 | tf_op jit(solution)/shard_map/ppermute | solution.py:21
  181.2 1.2 slice.82
  182.4 2.1 collective-permute-start.4
  184.6 0.0 collective-permute-done.3.refs_6_.refs_7_
  184.6 1.2 slice.83
  185.8 4.7 collective-permute-start.5
  190.6 3.3 fusion.39
  193.8 125.9 %collective-permute-done.refs_0_.refs_1_ = bf16[2560,1280]{1,0:T(8,128)(2,1)} collective-permute-done((bf16[2560,1280]{1,0:T(8,128)(2,1)}, bf16[2560,1280]{1,0:T(8,128)(2,1)}, u32[]{:S(2)}, u32[]{:S(2)}) %collective-permute-start) | collective-permute-done | bytes 6553632 | tf_op jit(solution)/shard_map/ppermute | solution.py:21
  319.7 5.4 collective-permute-done.1.refs_2_.refs_3_
  325.1 33.4 %collective-permute-done.4.refs_8_.refs_9_ = bf16[320,1280]{1,0:T(8,128)(2,1)S(1)} collective-permute-done((bf16[320,1280]{1,0:T(8,128)(2,1)S(1)}, bf16[320,1280]{1,0:T(8,128)(2,1)S(1)}, u32[]{:S(2)}, u32[]{:S(2)}) %collective-permute-start.4) | collective-permute-done | bytes 819232 | tf_op jit(solution)/shard_map/ppermute | solution.py:21
  358.6 0.9 copy-done.2
  359.5 0.3 copy-done.3
  359.7 40.8 %shard_map.65 = bf16[640,1280]{1,0:T(8,128)(2,1)} custom-call(s32[6,5]{1,0:T(8,128)} %get-tuple-element.46.t_ref, bf16[640,1280]{1,0:T(8,128)(2,1)} %get-tuple-element.32.q_ref, f32[640,1280]{1,0:T(8,128)} %get-tuple-element.30.acc1_ref, f32[640,10]{1,0:T(8,128)} %get-tuple-element.59.m1_ref, f32[640,10]{1,0:T(8,128)} %get-tuple-element.34.l1_ref, ...), custom_call_target="tpu_custom_call" | custom-call | flops 6710886400 | bytes 58982400 | tf_op jit(solution)/shard_map/pallas_call | solution.py:153
  400.5 4.8 convolution_convert_fusion.6
  405.3 4.2 convolution_convert_fusion.5
  409.6 0.3 pad_maximum_fusion.1
  409.9 0.1 collective-permute-start.6
  410.0 54.0 %shard_map.66 = bf16[640,1280]{1,0:T(8,128)(2,1)} custom-call(s32[6,5]{1,0:T(8,128)} %get-tuple-element.47.t_ref, bf16[640,1280]{1,0:T(8,128)(2,1)} %get-tuple-element.33.q_ref, f32[640,1280]{1,0:T(8,128)} %get-tuple-element.31.acc1_ref, f32[640,10]{1,0:T(8,128)} %get-tuple-element.58.m1_ref, f32[640,10]{1,0:T(8,128)} %get-tuple-element.35.l1_ref, ...), custom_call_target="tpu_custom_call" | custom-call | flops 6710886400 | bytes 58982400 | tf_op jit(solution)/shard_map/pallas_call | solution.py:153
  464.0 4.8 convolution_convert_fusion.2
  468.8 4.2 convolution_convert_fusion.1
  473.0 2.0 pad_maximum_fusion.2
  475.0 0.5 collective-permute-start.8
  475.5 4.8 convolution_convert_fusion.4
  480.4 2.0 fusion.12
  482.4 0.0 slice-start.4
  482.4 1.6 collective-permute-start.7
  484.0 4.2 convolution_convert_fusion
  488.2 1.9 fusion.13
  490.2 0.9 collective-permute-start.9
  491.1 2.3 convolution_convert_fusion.7
  493.4 2.3 convolution_convert_fusion.3
  495.7 25.5 %collective-permute-done.7 = bf16[1,640,1280]{2,1,0:T(8,128)(2,1)S(1)} collective-permute-done((bf16[1,640,1280]{2,1,0:T(8,128)(2,1)S(1)}, bf16[1,640,1280]{2,1,0:T(8,128)(2,1)S(1)}, u32[]{:S(2)}, u32[]{:S(2)}) %collective-permute-start.7) | collective-permute-done | bytes 1638432 | tf_op jit(solution)/shard_map/ppermute | solution.py:188
  521.2 2.0 fusion.2
  523.2 32.2 %collective-permute-done.9 = bf16[1,640,1280]{2,1,0:T(8,128)(2,1)S(1)} collective-permute-done((bf16[1,640,1280]{2,1,0:T(8,128)(2,1)S(1)}, bf16[1,640,1280]{2,1,0:T(8,128)(2,1)S(1)}, u32[]{:S(2)}, u32[]{:S(2)}) %collective-permute-start.9) | collective-permute-done | bytes 1638432 | tf_op jit(solution)/shard_map/ppermute | solution.py:188
  555.3 2.0 fusion
  557.4 1.9 pad_maximum_fusion.3
  (44 shorter events, 0.2 us)
Async XLA Ops:
  9.3 17.0 %copy-start = (bf16[1280,1280]{1,0:T(8,128)(2,1)S(1)}, bf16[1280,1280]{1,0:T(8,128)(2,1)}, u32[]{:S(2)}) copy-start(bf16[1280,1280]{1,0:T(8,128)(2,1)} %k_ref.1) | copy-start | bytes 9830404
  17.2 11.0 %copy-start.1 = (bf16[1280,1280]{1,0:T(8,128)(2,1)S(1)}, bf16[1280,1280]{1,0:T(8,128)(2,1)}, u32[]{:S(2)}) copy-start(bf16[1280,1280]{1,0:T(8,128)(2,1)} %v_ref.1) | copy-start | bytes 9830404
  17.2 164.0 %collective-permute-start.2 = (bf16[2880,1280]{1,0:T(8,128)(2,1)}, bf16[2880,1280]{1,0:T(8,128)(2,1)}, u32[]{:S(2)}, u32[]{:S(2)}) collective-permute-start(bf16[2880,1280]{1,0:T(8,128)(2,1)} %pad_maximum_fusion), channel_id=1, source_target_pairs={{8,0},{12,4},{16,8},{20,12},{24,16},{28,20},{9,1},{13,5},{17,9},{2... | collective-permute-start | bytes 22118408 | tf_op jit(solution)/shard_map/ppermute | solution.py:21
  19.8 164.8 %collective-permute-start.3 = (bf16[2880,1280]{1,0:T(8,128)(2,1)}, bf16[2880,1280]{1,0:T(8,128)(2,1)}, u32[]{:S(2)}, u32[]{:S(2)}) collective-permute-start(bf16[2880,1280]{1,0:T(8,128)(2,1)} %pad_maximum_fusion), channel_id=1, source_target_pairs={{0,8},{4,12},{8,16},{12,20},{16,24},{20,28},{1,9},{5,13},{9,17},{1... | collective-permute-start | bytes 22118408 | tf_op jit(solution)/shard_map/ppermute | solution.py:21
  28.1 7.8 %copy-start.10 = (s32[4]{0:T(128)S(1)}, s32[4]{0:T(128)}, u32[]{:S(2)}) copy-start(s32[4]{0:T(128)} %param.10) | copy-start | bytes 52
  28.1 11.1 %copy-start.9 = (s32[10,26]{1,0:T(8,128)S(1)}, s32[10,26]{1,0:T(8,128)}, u32[]{:S(2)}) copy-start(s32[10,26]{1,0:T(8,128)} %param.9) | copy-start | bytes 3124
  30.1 289.6 %collective-permute-start = (bf16[2560,1280]{1,0:T(8,128)(2,1)}, bf16[2560,1280]{1,0:T(8,128)(2,1)}, u32[]{:S(2)}, u32[]{:S(2)}) collective-permute-start(bf16[2560,1280]{1,0:T(8,128)(2,1)} %constant_dynamic-update-slice_fusion), channel_id=1, source_target_pairs={{4,0},{8,4},{12,8},{16,12},{20,16},{24,20},{28,24},{5,1},{9,5},{13... | collective-permute-start | bytes 19660808 | tf_op jit(solution)/shard_map/ppermute | solution.py:21
  32.0 293.1 %collective-permute-start.1 = (bf16[2560,1280]{1,0:T(8,128)(2,1)}, bf16[2560,1280]{1,0:T(8,128)(2,1)}, u32[]{:S(2)}, u32[]{:S(2)}) collective-permute-start(bf16[2560,1280]{1,0:T(8,128)(2,1)} %constant_dynamic-update-slice_fusion), channel_id=1, source_target_pairs={{0,4},{4,8},{8,12},{12,16},{16,20},{20,24},{24,28},{1,5},{5,9},{9,... | collective-permute-start | bytes 19660808 | tf_op jit(solution)/shard_map/ppermute | solution.py:21
  42.6 48.0 %copy-start.4 = (bf16[1280,1280]{1,0:T(8,128)(2,1)S(1)}, bf16[1280,1280]{1,0:T(8,128)(2,1)}, u32[]{:S(2)}) copy-start(bf16[1280,1280]{1,0:T(8,128)(2,1)} %q_ref.1) | copy-start | bytes 9830404
  88.1 102.4 %slice-start = ((s8[6553600]{0:T(1024)(128)(4,1)}), s8[4194304]{0:T(1024)(128)(4,1)S(1)}, s32[]{:S(2)}) async-start(s8[6553600]{0:T(1024)(128)(4,1)} %bitcast.66), calls=%async_computation | async-start | bytes 8388608
  90.6 99.9 %slice-start.1 = ((s8[6553600]{0:T(1024)(128)(4,1)}), s8[2359296]{0:T(1024)(128)(4,1)S(1)}, s32[]{:S(2)}) async-start(s8[6553600]{0:T(1024)(128)(4,1)} %bitcast.66), calls=%async_computation.1 | async-start | bytes 4718592
  182.4 176.1 %collective-permute-start.4 = (bf16[320,1280]{1,0:T(8,128)(2,1)S(1)}, bf16[320,1280]{1,0:T(8,128)(2,1)S(1)}, u32[]{:S(2)}, u32[]{:S(2)}) collective-permute-start(bf16[320,1280]{1,0:T(8,128)(2,1)S(1)} %slice.82), channel_id=1, source_target_pairs={{4,0},{8,4},{12,8},{16,12},{20,16},{24,20},{28,24},{5,1},{9,5},{13... | collective-permute-start | bytes 2457608 | tf_op jit(solution)/shard_map/ppermute | solution.py:21
  185.8 172.8 %collective-permute-start.5 = (bf16[320,1280]{1,0:T(8,128)(2,1)S(1)}, bf16[320,1280]{1,0:T(8,128)(2,1)S(1)}, u32[]{:S(2)}, u32[]{:S(2)}) collective-permute-start(bf16[320,1280]{1,0:T(8,128)(2,1)S(1)} %slice.83), channel_id=1, source_target_pairs={{0,4},{4,8},{8,12},{12,16},{16,20},{20,24},{24,28},{1,5},{5,9},{9,... | collective-permute-start | bytes 2457608 | tf_op jit(solution)/shard_map/ppermute | solution.py:21
  358.5 0.9 copy-start.2
  358.6 1.2 copy-start.3
  400.5 4.8 copy-start.5
  409.9 70.5 %collective-permute-start.6 = (bf16[2,640,1280]{2,1,0:T(8,128)(2,1)S(1)}, bf16[2,640,1280]{2,1,0:T(8,128)(2,1)}, u32[]{:S(2)}, u32[]{:S(2)}) collective-permute-start(bf16[2,640,1280]{2,1,0:T(8,128)(2,1)S(1)} %pad_maximum_fusion.1), channel_id=1, source_target_pairs={{0,1},{1,0},{2,3},{3,2},{4,5},{5,4},{6,7},{7,6},{8,9},{9,8},{10,11... | collective-permute-start | bytes 9830408 | tf_op jit(solution)/shard_map/ppermute | solution.py:188
  463.9 4.8 copy-start.7
  475.0 13.2 %collective-permute-start.8 = (bf16[2,640,1280]{2,1,0:T(8,128)(2,1)}, bf16[2,640,1280]{2,1,0:T(8,128)(2,1)}, u32[]{:S(2)}, u32[]{:S(2)}) collective-permute-start(bf16[2,640,1280]{2,1,0:T(8,128)(2,1)} %pad_maximum_fusion.2), channel_id=1, source_target_pairs={{0,1},{1,0},{2,3},{3,2},{4,5},{5,4},{6,7},{7,6},{8,9},{9,8},{10,11... | collective-permute-start | bytes 9830408 | tf_op jit(solution)/shard_map/ppermute | solution.py:188
  475.5 15.5 %slice-start.2 = ((s8[13107200]{0:T(1024)(128)(4,1)}), s8[4194304]{0:T(1024)(128)(4,1)S(1)}, s32[]{:S(2)}) async-start(s8[13107200]{0:T(1024)(128)(4,1)} %bitcast.72), calls=%async_computation.2 | async-start | bytes 8388608
  475.5 15.5 %slice-start.3 = ((s8[13107200]{0:T(1024)(128)(4,1)}), s8[4194304]{0:T(1024)(128)(4,1)S(1)}, s32[]{:S(2)}) async-start(s8[13107200]{0:T(1024)(128)(4,1)} %bitcast.72), calls=%async_computation.3 | async-start | bytes 8388608
  480.4 3.6 copy-start.8
  482.4 8.7 %slice-start.4 = ((s8[13107200]{0:T(1024)(128)(4,1)}), s8[4194304]{0:T(1024)(128)(4,1)S(1)}, s32[]{:S(2)}) async-start(s8[13107200]{0:T(1024)(128)(4,1)} %bitcast.72), calls=%async_computation.4 | async-start | bytes 8388608
  482.4 8.6 %slice-start.5 = ((s8[13107200]{0:T(1024)(128)(4,1)}), s8[524288]{0:T(1024)(128)(4,1)S(1)}, s32[]{:S(2)}) async-start(s8[13107200]{0:T(1024)(128)(4,1)} %bitcast.72), calls=%async_computation.5 | async-start | bytes 1048576
  482.4 38.7 %collective-permute-start.7 = (bf16[1,640,1280]{2,1,0:T(8,128)(2,1)S(1)}, bf16[1,640,1280]{2,1,0:T(8,128)(2,1)S(1)}, u32[]{:S(2)}, u32[]{:S(2)}) collective-permute-start(bf16[1,640,1280]{2,1,0:T(8,128)(2,1)S(1)} %fusion.12), channel_id=1, source_target_pairs={{0,2},{1,3},{2,0},{3,1},{4,6},{5,7},{6,4},{7,5},{8,10},{9,11},{10,... | collective-permute-start | bytes 4915208 | tf_op jit(solution)/shard_map/ppermute | solution.py:188
  488.2 2.8 copy-start.6
  490.2 65.2 %collective-permute-start.9 = (bf16[1,640,1280]{2,1,0:T(8,128)(2,1)S(1)}, bf16[1,640,1280]{2,1,0:T(8,128)(2,1)S(1)}, u32[]{:S(2)}, u32[]{:S(2)}) collective-permute-start(bf16[1,640,1280]{2,1,0:T(8,128)(2,1)S(1)} %fusion.13), channel_id=1, source_target_pairs={{0,2},{1,3},{2,0},{3,1},{4,6},{5,7},{6,4},{7,5},{8,10},{9,11},{10,... | collective-permute-start | bytes 4915208 | tf_op jit(solution)/shard_map/ppermute | solution.py:188

commit v4 on v3

--- a/solution.py
+++ b/solution.py
@@ -61,15 +61,23 @@
 
 
 def own_kernel(q_ref, k_ref, v_ref, acc_ref, m_ref, l_ref, *, heads, scale):
-    for h in range(heads):
-        cols = pl.ds(h * HD, HD)
+    lanes = lax.broadcasted_iota(jnp.int32, (BLK, heads), 1)
+
+    def one_head(h, carry):
+        m_all, l_all = carry
+        cols = pl.ds(pl.multiple_of(h * HD, HD), HD)
         sc = lax.dot_general(q_ref[:, cols], k_ref[:, cols], (((1,), (1,)), ((), ())), preferred_element_type=jnp.float32)
         sc = sc * scale
         m = jnp.max(sc, axis=1, keepdims=True)
         p = jnp.exp(sc - m)
-        m_ref[:, h:h + 1] = m
-        l_ref[:, h:h + 1] = jnp.sum(p, axis=1, keepdims=True)
         acc_ref[:, cols] = jnp.dot(p.astype(jnp.bfloat16), v_ref[:, cols], preferred_element_type=jnp.float32)
+        pick = lanes == h
+        return jnp.where(pick, m, m_all), jnp.where(pick, jnp.sum(p, axis=1, keepdims=True), l_all)
+
+    zero = jnp.zeros((BLK, heads), jnp.float32)
+    m_all, l_all = lax.fori_loop(0, heads, one_head, (zero, zero))
+    m_ref[...] = m_all
+    l_ref[...] = l_all
 
 
 def attend_own(query, key_act, value_act):

time: 559 us -> 547 us (0.979)
  waiting for transfers between devices: 311 us -> 290 us
  Pallas kernels: 140 us -> 149 us
    pallas_call x1, Pallas kernels: 45.5 us -> 66.7 us  [attend_own(): pl.pallas_call(kernel, out_shape=(jax.ShapeDtypeStruct((rows, width), jnp...]
    ppermute x6, waiting for transfers between devices: 253 us -> 232 us  [from_behind(): return lax.ppermute(shard, axis, pairs)]
    pallas_call x2, Pallas kernels: 94.7 us -> 81.8 us  [attend(): pl.pallas_call(kernel, out_shape=jax.ShapeDtypeStruct(query.shape, jnp.bf...]
  transfers between devices with their start and end apart: 10 -> 10, of which waited for: 6 -> 6; matrix products, arithmetic and copies ran while one was open for 9% -> 9% of each run, Pallas kernels for 18% -> 20%
where the time goes in v4:
time: 547 us; the launch traced here: 546 us
  waiting for transfers between devices  290 us (53%)
  Pallas kernels  149 us (27%)
  matrix products  31.7 us (6%)
  local copies, waits for them, and re-layouts  27.1 us (5%)
  starting transfers between devices  24.6 us (4%)
  other arithmetic  21.4 us (4%)
    ppermute x6, waiting for transfers between devices, from_behind(): return lax.ppermute(shard, axis, pairs)  232 us
    pallas_call x2, Pallas kernels, attend(): pl.pallas_call(kernel, out_shape=jax.ShapeDtypeStruct(query.shape, jnp.bf...  81.8 us
    pallas_call x1, Pallas kernels, attend_own(): pl.pallas_call(kernel, out_shape=(jax.ShapeDtypeStruct((rows, width), jnp...  66.7 us
    ppermute x4, waiting for transfers between devices, halving_scatter(): got = lax.ppermute(payload, axis, pairs)  57.6 us
    dot_general x8, matrix products, term(): t = jnp.dot(attended, cols, preferred_element_type=jnp.float32)  31.7 us
    ppermute x6, starting transfers between devices, from_behind(): return lax.ppermute(shard, axis, pairs)  21.7 us
  transfers between devices with their start and end apart: 10, of which 6 were waited for; matrix products, arithmetic and copies ran while one was open for 9% of the time, Pallas kernels for 20%

profile of v4, /device:TPU:16, one launch (start us, length us, event | category | flops | bytes accessed | tf_op | source)
XLA Modules:
  0.0 546.3 jit_solution(17190472875154077899)
XLA Ops:
  0.0 4.6 slice.67
  4.6 4.6 slice.68
  9.3 0.0 copy-start
  9.3 7.9 %pad_maximum_fusion = bf16[2880,1280]{1,0:T(8,128)(2,1)} fusion(bf16[160,1280]{1,0:T(8,128)(2,1)S(1)} %slice.68, bf16[160,1280]{1,0:T(8,128)(2,1)S(1)} %slice.67, bf16[1280,1280]{1,0:T(8,128)(2,1)} %v_ref.1, bf16[1280,1280]{1,0:T(8,128)(2,1)} %k_ref.1), kind=kLoop, calls=%fused_computation | loop fusion | flops 29491200 | bytes 14745600 | tf_op jit(solution)/shard_map/concatenate | solution.py:34
  17.2 2.6 collective-permute-start.2
  19.8 6.4 %collective-permute-start.3 = (bf16[2880,1280]{1,0:T(8,128)(2,1)}, bf16[2880,1280]{1,0:T(8,128)(2,1)}, u32[]{:S(2)}, u32[]{:S(2)}) collective-permute-start(bf16[2880,1280]{1,0:T(8,128)(2,1)} %pad_maximum_fusion), channel_id=1, source_target_pairs={{0,8},{4,12},{8,16},{12,20},{16,24},{20,28},{1,9},{5,13},{9,17},{1... | collective-permute-start | bytes 22118408 | tf_op jit(solution)/shard_map/ppermute | solution.py:21
  26.2 1.9 constant_dynamic-update-slice_fusion.1
  28.2 2.0 constant_dynamic-update-slice_fusion
  30.1 1.9 collective-permute-start
  32.0 3.9 collective-permute-start.1
  36.0 0.7 fusion.44
  39.3 0.1 fusion.33
  39.4 0.1 fusion.35
  39.5 0.2 select_reduce_fusion
  39.7 0.1 reduce_or.66
  39.9 0.1 fusion.31
  40.0 0.1 and_dynamic-update-slice_fusion.1
  40.1 0.1 and_dynamic-update-slice_fusion
  40.2 0.1 constant_dynamic-update-slice_fusion.5
  40.3 0.1 constant_dynamic-update-slice_fusion.4
  40.3 0.1 constant_dynamic-update-slice_fusion.3
  40.4 0.1 constant_dynamic-update-slice_fusion.2
  40.5 0.7 copy.7.refs_12_
  41.2 0.6 slice.81.refs_12_
  41.9 0.7 fusion.43
  42.6 66.7 %shard_map.64 = (f32[1280,1280]{1,0:T(8,128)}, f32[1280,10]{1,0:T(8,128)}, f32[1280,10]{1,0:T(8,128)}) custom-call(bf16[1280,1280]{1,0:T(8,128)(2,1)} %q_ref.1, bf16[1280,1280]{1,0:T(8,128)(2,1)} %k_ref.1, bf16[1280,1280]{1,0:T(8,128)(2,1)} %v_ref.1), custom_call_target="tpu_custom_call" | custom-call | flops 8388608000 | bytes 16384000 | tf_op jit(solution)/shard_map/pallas_call | solution.py:90
  109.3 2.5 fusion.41
  111.9 1.9 fusion.40
  113.8 67.4 %collective-permute-done.2.refs_4_.refs_5_ = bf16[2880,1280]{1,0:T(8,128)(2,1)} collective-permute-done((bf16[2880,1280]{1,0:T(8,128)(2,1)}, bf16[2880,1280]{1,0:T(8,128)(2,1)}, u32[]{:S(2)}, u32[]{:S(2)}) %collective-permute-start.2) | collective-permute-done | bytes 7372832 | tf_op jit(solution)/shard_map/ppermute | solution.py:21
  181.2 1.2 slice.82
  182.4 2.1 collective-permute-start.4
  184.6 0.0 collective-permute-done.3.refs_6_.refs_7_
  184.6 1.2 slice.83
  185.8 4.7 collective-permute-start.5
  190.5 3.3 fusion.39
  193.7 125.9 %collective-permute-done.refs_0_.refs_1_ = bf16[2560,1280]{1,0:T(8,128)(2,1)} collective-permute-done((bf16[2560,1280]{1,0:T(8,128)(2,1)}, bf16[2560,1280]{1,0:T(8,128)(2,1)}, u32[]{:S(2)}, u32[]{:S(2)}) %collective-permute-start) | collective-permute-done | bytes 6553632 | tf_op jit(solution)/shard_map/ppermute | solution.py:21
  319.7 5.4 collective-permute-done.1.refs_2_.refs_3_
  325.1 33.4 %collective-permute-done.4.refs_8_.refs_9_ = bf16[320,1280]{1,0:T(8,128)(2,1)S(1)} collective-permute-done((bf16[320,1280]{1,0:T(8,128)(2,1)S(1)}, bf16[320,1280]{1,0:T(8,128)(2,1)S(1)}, u32[]{:S(2)}, u32[]{:S(2)}) %collective-permute-start.4) | collective-permute-done | bytes 819232 | tf_op jit(solution)/shard_map/ppermute | solution.py:21
  358.6 0.9 copy-done.2
  359.5 0.3 copy-done.3
  359.7 40.8 %shard_map.65 = bf16[640,1280]{1,0:T(8,128)(2,1)} custom-call(s32[6,5]{1,0:T(8,128)} %get-tuple-element.46.t_ref, bf16[640,1280]{1,0:T(8,128)(2,1)} %get-tuple-element.32.q_ref, f32[640,1280]{1,0:T(8,128)} %get-tuple-element.30.acc1_ref, f32[640,10]{1,0:T(8,128)} %get-tuple-element.59.m1_ref, f32[640,10]{1,0:T(8,128)} %get-tuple-element.34.l1_ref, ...), custom_call_target="tpu_custom_call" | custom-call | flops 6710886400 | bytes 58982400 | tf_op jit(solution)/shard_map/pallas_call | solution.py:161
  400.5 4.8 convolution_convert_fusion.6
  405.4 4.2 convolution_convert_fusion.5
  409.6 0.3 pad_maximum_fusion.1
  409.9 0.1 collective-permute-start.6
  410.0 41.0 %shard_map.66 = bf16[640,1280]{1,0:T(8,128)(2,1)} custom-call(s32[6,5]{1,0:T(8,128)} %get-tuple-element.47.t_ref, bf16[640,1280]{1,0:T(8,128)(2,1)} %get-tuple-element.33.q_ref, f32[640,1280]{1,0:T(8,128)} %get-tuple-element.31.acc1_ref, f32[640,10]{1,0:T(8,128)} %get-tuple-element.58.m1_ref, f32[640,10]{1,0:T(8,128)} %get-tuple-element.35.l1_ref, ...), custom_call_target="tpu_custom_call" | custom-call | flops 6710886400 | bytes 58982400 | tf_op jit(solution)/shard_map/pallas_call | solution.py:161
  451.0 4.8 convolution_convert_fusion.2
  455.8 4.2 convolution_convert_fusion.1
  460.1 2.0 pad_maximum_fusion.2
  462.0 0.5 collective-permute-start.8
  462.5 4.8 convolution_convert_fusion.4
  467.4 2.0 fusion.12
  469.4 0.0 slice-start.4
  469.4 1.6 collective-permute-start.7
  471.0 4.2 convolution_convert_fusion
  475.3 1.9 fusion.13
  477.2 0.9 collective-permute-start.9
  478.1 2.3 convolution_convert_fusion.7
  480.4 2.3 convolution_convert_fusion.3
  482.7 25.5 %collective-permute-done.7 = bf16[1,640,1280]{2,1,0:T(8,128)(2,1)S(1)} collective-permute-done((bf16[1,640,1280]{2,1,0:T(8,128)(2,1)S(1)}, bf16[1,640,1280]{2,1,0:T(8,128)(2,1)S(1)}, u32[]{:S(2)}, u32[]{:S(2)}) %collective-permute-start.7) | collective-permute-done | bytes 1638432 | tf_op jit(solution)/shard_map/ppermute | solution.py:196
  508.2 2.0 fusion.2
  510.2 32.2 %collective-permute-done.9 = bf16[1,640,1280]{2,1,0:T(8,128)(2,1)S(1)} collective-permute-done((bf16[1,640,1280]{2,1,0:T(8,128)(2,1)S(1)}, bf16[1,640,1280]{2,1,0:T(8,128)(2,1)S(1)}, u32[]{:S(2)}, u32[]{:S(2)}) %collective-permute-start.9) | collective-permute-done | bytes 1638432 | tf_op jit(solution)/shard_map/ppermute | solution.py:196
  542.4 2.0 fusion
  544.4 1.9 pad_maximum_fusion.3
  (44 shorter events, 0.2 us)
Async XLA Ops:
  9.3 17.0 %copy-start = (bf16[1280,1280]{1,0:T(8,128)(2,1)S(1)}, bf16[1280,1280]{1,0:T(8,128)(2,1)}, u32[]{:S(2)}) copy-start(bf16[1280,1280]{1,0:T(8,128)(2,1)} %k_ref.1) | copy-start | bytes 9830404
  17.2 11.0 %copy-start.1 = (bf16[1280,1280]{1,0:T(8,128)(2,1)S(1)}, bf16[1280,1280]{1,0:T(8,128)(2,1)}, u32[]{:S(2)}) copy-start(bf16[1280,1280]{1,0:T(8,128)(2,1)} %v_ref.1) | copy-start | bytes 9830404
  17.2 164.0 %collective-permute-start.2 = (bf16[2880,1280]{1,0:T(8,128)(2,1)}, bf16[2880,1280]{1,0:T(8,128)(2,1)}, u32[]{:S(2)}, u32[]{:S(2)}) collective-permute-start(bf16[2880,1280]{1,0:T(8,128)(2,1)} %pad_maximum_fusion), channel_id=1, source_target_pairs={{8,0},{12,4},{16,8},{20,12},{24,16},{28,20},{9,1},{13,5},{17,9},{2... | collective-permute-start | bytes 22118408 | tf_op jit(solution)/shard_map/ppermute | solution.py:21
  19.8 164.8 %collective-permute-start.3 = (bf16[2880,1280]{1,0:T(8,128)(2,1)}, bf16[2880,1280]{1,0:T(8,128)(2,1)}, u32[]{:S(2)}, u32[]{:S(2)}) collective-permute-start(bf16[2880,1280]{1,0:T(8,128)(2,1)} %pad_maximum_fusion), channel_id=1, source_target_pairs={{0,8},{4,12},{8,16},{12,20},{16,24},{20,28},{1,9},{5,13},{9,17},{1... | collective-permute-start | bytes 22118408 | tf_op jit(solution)/shard_map/ppermute | solution.py:21
  28.1 7.8 %copy-start.10 = (s32[4]{0:T(128)S(1)}, s32[4]{0:T(128)}, u32[]{:S(2)}) copy-start(s32[4]{0:T(128)} %param.10) | copy-start | bytes 52
  28.1 11.1 %copy-start.9 = (s32[10,26]{1,0:T(8,128)S(1)}, s32[10,26]{1,0:T(8,128)}, u32[]{:S(2)}) copy-start(s32[10,26]{1,0:T(8,128)} %param.9) | copy-start | bytes 3124
  30.1 289.6 %collective-permute-start = (bf16[2560,1280]{1,0:T(8,128)(2,1)}, bf16[2560,1280]{1,0:T(8,128)(2,1)}, u32[]{:S(2)}, u32[]{:S(2)}) collective-permute-start(bf16[2560,1280]{1,0:T(8,128)(2,1)} %constant_dynamic-update-slice_fusion), channel_id=1, source_target_pairs={{4,0},{8,4},{12,8},{16,12},{20,16},{24,20},{28,24},{5,1},{9,5},{13... | collective-permute-start | bytes 19660808 | tf_op jit(solution)/shard_map/ppermute | solution.py:21
  32.0 293.1 %collective-permute-start.1 = (bf16[2560,1280]{1,0:T(8,128)(2,1)}, bf16[2560,1280]{1,0:T(8,128)(2,1)}, u32[]{:S(2)}, u32[]{:S(2)}) collective-permute-start(bf16[2560,1280]{1,0:T(8,128)(2,1)} %constant_dynamic-update-slice_fusion), channel_id=1, source_target_pairs={{0,4},{4,8},{8,12},{12,16},{16,20},{20,24},{24,28},{1,5},{5,9},{9,... | collective-permute-start | bytes 19660808 | tf_op jit(solution)/shard_map/ppermute | solution.py:21
  42.6 69.3 %copy-start.4 = (bf16[1280,1280]{1,0:T(8,128)(2,1)S(1)}, bf16[1280,1280]{1,0:T(8,128)(2,1)}, u32[]{:S(2)}) copy-start(bf16[1280,1280]{1,0:T(8,128)(2,1)} %q_ref.1) | copy-start | bytes 9830404
  109.3 81.1 %slice-start = ((s8[6553600]{0:T(1024)(128)(4,1)}), s8[4194304]{0:T(1024)(128)(4,1)S(1)}, s32[]{:S(2)}) async-start(s8[6553600]{0:T(1024)(128)(4,1)} %bitcast.66), calls=%async_computation | async-start | bytes 8388608
  111.9 78.6 %slice-start.1 = ((s8[6553600]{0:T(1024)(128)(4,1)}), s8[2359296]{0:T(1024)(128)(4,1)S(1)}, s32[]{:S(2)}) async-start(s8[6553600]{0:T(1024)(128)(4,1)} %bitcast.66), calls=%async_computation.1 | async-start | bytes 4718592
  182.4 176.1 %collective-permute-start.4 = (bf16[320,1280]{1,0:T(8,128)(2,1)S(1)}, bf16[320,1280]{1,0:T(8,128)(2,1)S(1)}, u32[]{:S(2)}, u32[]{:S(2)}) collective-permute-start(bf16[320,1280]{1,0:T(8,128)(2,1)S(1)} %slice.82), channel_id=1, source_target_pairs={{4,0},{8,4},{12,8},{16,12},{20,16},{24,20},{28,24},{5,1},{9,5},{13... | collective-permute-start | bytes 2457608 | tf_op jit(solution)/shard_map/ppermute | solution.py:21
  185.8 172.8 %collective-permute-start.5 = (bf16[320,1280]{1,0:T(8,128)(2,1)S(1)}, bf16[320,1280]{1,0:T(8,128)(2,1)S(1)}, u32[]{:S(2)}, u32[]{:S(2)}) collective-permute-start(bf16[320,1280]{1,0:T(8,128)(2,1)S(1)} %slice.83), channel_id=1, source_target_pairs={{0,4},{4,8},{8,12},{12,16},{16,20},{20,24},{24,28},{1,5},{5,9},{9,... | collective-permute-start | bytes 2457608 | tf_op jit(solution)/shard_map/ppermute | solution.py:21
  358.5 0.9 copy-start.2
  358.6 1.2 copy-start.3
  400.5 4.8 copy-start.5
  409.9 57.5 %collective-permute-start.6 = (bf16[2,640,1280]{2,1,0:T(8,128)(2,1)S(1)}, bf16[2,640,1280]{2,1,0:T(8,128)(2,1)}, u32[]{:S(2)}, u32[]{:S(2)}) collective-permute-start(bf16[2,640,1280]{2,1,0:T(8,128)(2,1)S(1)} %pad_maximum_fusion.1), channel_id=1, source_target_pairs={{0,1},{1,0},{2,3},{3,2},{4,5},{5,4},{6,7},{7,6},{8,9},{9,8},{10,11... | collective-permute-start | bytes 9830408 | tf_op jit(solution)/shard_map/ppermute | solution.py:196
  451.0 4.8 copy-start.7
  462.0 13.2 %collective-permute-start.8 = (bf16[2,640,1280]{2,1,0:T(8,128)(2,1)}, bf16[2,640,1280]{2,1,0:T(8,128)(2,1)}, u32[]{:S(2)}, u32[]{:S(2)}) collective-permute-start(bf16[2,640,1280]{2,1,0:T(8,128)(2,1)} %pad_maximum_fusion.2), channel_id=1, source_target_pairs={{0,1},{1,0},{2,3},{3,2},{4,5},{5,4},{6,7},{7,6},{8,9},{9,8},{10,11... | collective-permute-start | bytes 9830408 | tf_op jit(solution)/shard_map/ppermute | solution.py:196
  462.5 15.6 %slice-start.2 = ((s8[13107200]{0:T(1024)(128)(4,1)}), s8[4194304]{0:T(1024)(128)(4,1)S(1)}, s32[]{:S(2)}) async-start(s8[13107200]{0:T(1024)(128)(4,1)} %bitcast.72), calls=%async_computation.2 | async-start | bytes 8388608
  462.5 15.6 %slice-start.3 = ((s8[13107200]{0:T(1024)(128)(4,1)}), s8[4194304]{0:T(1024)(128)(4,1)S(1)}, s32[]{:S(2)}) async-start(s8[13107200]{0:T(1024)(128)(4,1)} %bitcast.72), calls=%async_computation.3 | async-start | bytes 8388608
  467.4 3.6 copy-start.8
  469.4 8.7 %slice-start.4 = ((s8[13107200]{0:T(1024)(128)(4,1)}), s8[4194304]{0:T(1024)(128)(4,1)S(1)}, s32[]{:S(2)}) async-start(s8[13107200]{0:T(1024)(128)(4,1)} %bitcast.72), calls=%async_computation.4 | async-start | bytes 8388608
  469.4 8.7 %slice-start.5 = ((s8[13107200]{0:T(1024)(128)(4,1)}), s8[524288]{0:T(1024)(128)(4,1)S(1)}, s32[]{:S(2)}) async-start(s8[13107200]{0:T(1024)(128)(4,1)} %bitcast.72), calls=%async_computation.5 | async-start | bytes 1048576
  469.4 38.7 %collective-permute-start.7 = (bf16[1,640,1280]{2,1,0:T(8,128)(2,1)S(1)}, bf16[1,640,1280]{2,1,0:T(8,128)(2,1)S(1)}, u32[]{:S(2)}, u32[]{:S(2)}) collective-permute-start(bf16[1,640,1280]{2,1,0:T(8,128)(2,1)S(1)} %fusion.12), channel_id=1, source_target_pairs={{0,2},{1,3},{2,0},{3,1},{4,6},{5,7},{6,4},{7,5},{8,10},{9,11},{10,... | collective-permute-start | bytes 4915208 | tf_op jit(solution)/shard_map/ppermute | solution.py:196
  475.2 2.9 copy-start.6
  477.2 65.2 %collective-permute-start.9 = (bf16[1,640,1280]{2,1,0:T(8,128)(2,1)S(1)}, bf16[1,640,1280]{2,1,0:T(8,128)(2,1)S(1)}, u32[]{:S(2)}, u32[]{:S(2)}) collective-permute-start(bf16[1,640,1280]{2,1,0:T(8,128)(2,1)S(1)} %fusion.13), channel_id=1, source_target_pairs={{0,2},{1,3},{2,0},{3,1},{4,6},{5,7},{6,4},{7,5},{8,10},{9,11},{10,... | collective-permute-start | bytes 4915208 | tf_op jit(solution)/shard_map/ppermute | solution.py:196
